TPU v7x, 32 devices: a whole 2x2x4 slice. The times are simulated.
32 devices in a mesh: grp: 2 (over y), seq: 4 (over z), head: 4 (over x, core).
Axes of the slice: x: 2, y: 2, z: 4, core: 2. Of those that a mesh axis runs over, the one named last changes fastest.
Arguments:
- queries: bfloat16 [4096, 8, 512], P(('grp', 'seq'), 'head'), parts along dimension 0, may hold values from -30 to 30
- keys: bfloat16 [4096, 8, 128], P(('grp', 'seq'), 'head'), parts along dimension 0, may hold values from -30 to 30
- values: bfloat16 [4096, 8, 128], P(('grp', 'seq'), 'head'), parts along dimension 0, may hold values from -6 to 6
- doc_blocks: int32 [8], P('grp'), parts along dimension 0, may hold values from 1 to 8, 16 in all
Outputs:
- attended: bfloat16 [4096, 8, 512], P(('grp', 'seq'), 'head'), parts along dimension 0
There are 2 independent parts, one for each index of `grp`. A program takes and returns all parts, laid end to end along the dimension named above; each array names one. Nothing has to cross between parts.
Inputs may be any that keep to these rules, and one draw needn't show every extreme that they name: `doc_blocks`: each document spans whole blocks; the longest has exactly 8 blocks and the lengths sum to 16.
All inputs are finite; a program needn't handle non-finite values.
Results may differ from a plain program's by a relative error of at most 0.0036.
Values may be sent and summed in bfloat16 or wider, within the bound.
No kernel may reach another device: no remote copies, remote signals or barrier semaphores. Data moves between devices by JAX's collectives and lax.ppermute only.
A program may use at most 64 MiB of HBM per device.

v0:
```python
import jax
import jax.numpy as jnp
from jax import lax
from jax.experimental import pallas as pl
from jax.experimental.pallas import tpu as pltpu
from jax.sharding import PartitionSpec as P


BLK = 128


def shift_up(block, axis):
    size = lax.axis_size(axis)
    return lax.ppermute(block, axis, [(i, i + 1) for i in range(size - 1)])


def first_needed(distance, reach, dev_blocks):
    return max(0, (distance - reach) * dev_blocks + 1)


def stage_regions(stage, i, dev_blocks, doc_blk, firsts):
    if stage == 0:
        lo, hi = 0, i
    else:
        lo = -stage * dev_blocks + firsts[stage]
        hi = -(stage - 1) * dev_blocks - 1
    lo = max(lo, i - doc_blk + 1)
    rels = list(range(lo, hi + 1))
    regions = []
    while rels:
        take = 2 if len(rels) % 2 == 0 else 1
        regions.append(rels[:take])
        rels = rels[take:]
    return regions


def make_stage(stage, first, last, dev_blocks, doc_blk, firsts, groups, head_dim, score_scale):
    def local_index(rel):
        if stage == 0:
            return rel
        return rel + stage * dev_blocks - firsts[stage]

    def kernel(rel_ref, q_ref, k_ref, v_ref, *refs):
        if first:
            acc_in = m_in = l_in = None
            rest = refs
        else:
            acc_in, m_in, l_in = refs[:3]
            rest = refs[3:]
        if last:
            o_ref = rest[0]
            s_sc, m_sc, l_sc, acc_sc = rest[1:]
        else:
            acc_out, m_out, l_out = rest[:3]
            s_sc, m_sc, l_sc, acc_sc = rest[3:]

        for i in range(dev_blocks):
            start = rel_ref[i]
            regions = stage_regions(stage, i, dev_blocks, doc_blk, firsts)
            if first:
                m_old = jnp.full((1, groups * BLK), -jnp.inf, jnp.float32)
                l_old = jnp.zeros((1, groups * BLK), jnp.float32)
            else:
                m_old = m_in[i : i + 1, :]
                l_old = l_in[i : i + 1, :]
            m_sc[...] = m_old
            if not regions:
                m_new = m_old
                l_sc[...] = l_old
                if first:
                    acc_sc[...] = jnp.zeros(acc_sc.shape, jnp.float32)
                else:
                    acc_sc[...] = acc_in[i]
            else:
                q = jnp.concatenate(
                    [q_ref[i * BLK : (i + 1) * BLK, g * head_dim : (g + 1) * head_dim] for g in range(groups)],
                    axis=0,
                )

                def scores(rels):
                    lo = local_index(rels[0])
                    k = k_ref[lo * BLK : (lo + len(rels)) * BLK, :]
                    s = lax.dot_general(
                        k, q, (((1,), (1,)), ((), ())), preferred_element_type=jnp.float32
                    ) * score_scale
                    if rels[-1] == i:
                        key = lax.broadcasted_iota(jnp.int32, s.shape, 0) + (rels[0] - i) * BLK
                        tok = lax.broadcasted_iota(jnp.int32, s.shape, 1) % BLK
                        s = jnp.where(key <= tok, s, -jnp.inf)
                    return s

                def variants(rels):
                    out = [(rels, start <= rels[0])]
                    if len(rels) == 2:
                        out.append((rels[1:], start == rels[1]))
                    return out

                for r, rels in enumerate(regions):
                    for sub, cond in variants(rels):
                        @pl.when(cond)
                        def _():
                            s = scores(sub)
                            s_sc[r, : len(sub) * BLK, :] = s
                            m_sc[...] = jnp.maximum(m_sc[...], jnp.max(s, axis=0, keepdims=True))

                m_new = m_sc[...]
                alpha = jnp.exp(m_old - m_new)
                l_sc[...] = alpha * l_old
                if first:
                    acc_sc[...] = jnp.zeros(acc_sc.shape, jnp.float32)
                else:
                    acc_sc[...] = alpha * acc_in[i]

                for r, rels in enumerate(regions):
                    for sub, cond in variants(rels):
                        @pl.when(cond)
                        def _():
                            p = jnp.exp(s_sc[r, : len(sub) * BLK, :] - m_new)
                            l_sc[...] = l_sc[...] + jnp.sum(p, axis=0, keepdims=True)
                            lo = local_index(sub[0])
                            v = v_ref[lo * BLK : (lo + len(sub)) * BLK, :]
                            acc_sc[...] = acc_sc[...] + lax.dot_general(
                                v, p.astype(jnp.bfloat16), (((0,), (0,)), ((), ())),
                                preferred_element_type=jnp.float32,
                            )

            if last:
                out_t = acc_sc[...] / l_sc[...]
                out = jnp.transpose(out_t)
                for g in range(groups):
                    o_ref[i * BLK : (i + 1) * BLK, g * head_dim : (g + 1) * head_dim] = out[
                        g * BLK : (g + 1) * BLK
                    ].astype(o_ref.dtype)
            else:
                acc_out[i] = acc_sc[...]
                m_out[i : i + 1, :] = m_new if regions else m_old
                l_out[i : i + 1, :] = l_sc[...]

    return kernel


def doc_start_of(doc_blocks, blocks):
    ends = jnp.cumsum(doc_blocks)
    starts = ends - doc_blocks
    return jnp.max(jnp.where(starts[None, :] <= blocks[:, None], starts[None, :], 0), axis=1)


def on_device(queries, keys, values, doc_blocks):
    tok_rows, heads, qwidth = queries.shape
    head_dim = keys.shape[2]
    groups = qwidth // head_dim
    rows = groups * BLK
    dev_blocks = tok_rows // BLK
    score_scale = head_dim ** (-0.5)
    reach = min(4, lax.axis_size("seq") // 2)
    doc_blk = reach * dev_blocks
    firsts = [0] + [first_needed(r, reach, dev_blocks) for r in range(1, reach + 1)]

    device_pos = lax.axis_index("seq")
    first_block = device_pos * dev_blocks
    q_blocks = first_block + jnp.arange(dev_blocks, dtype=jnp.int32)
    rel_start = (doc_start_of(doc_blocks, q_blocks) - first_block).astype(jnp.int32)

    q2 = queries.reshape(tok_rows, heads * qwidth)
    k2 = keys.reshape(tok_rows, heads * head_dim)
    v2 = values.reshape(tok_rows, heads * head_dim)

    k_src, v_src = [k2], [v2]
    k_cur, v_cur = k2, v2
    prev_first = 0
    for r in range(1, reach + 1):
        cut = (firsts[r] - prev_first) * BLK
        k_cur, v_cur = shift_up((k_cur[cut:], v_cur[cut:]), "seq")
        prev_first = firsts[r]
        k_src.append(k_cur)
        v_src.append(v_cur)

    state_shapes = (
        jax.ShapeDtypeStruct((heads, dev_blocks, head_dim, rows), jnp.float32),
        jax.ShapeDtypeStruct((heads, dev_blocks, rows), jnp.float32),
        jax.ShapeDtypeStruct((heads, dev_blocks, rows), jnp.float32),
    )
    state_specs = [
        pl.BlockSpec((None, dev_blocks, head_dim, rows), lambda h, rel: (h, 0, 0, 0)),
        pl.BlockSpec((None, dev_blocks, rows), lambda h, rel: (h, 0, 0)),
        pl.BlockSpec((None, dev_blocks, rows), lambda h, rel: (h, 0, 0)),
    ]
    scratch = [
        pltpu.VMEM((max(1, (dev_blocks + 1) // 2), 2 * BLK, rows), jnp.float32),
        pltpu.VMEM((1, rows), jnp.float32),
        pltpu.VMEM((1, rows), jnp.float32),
        pltpu.VMEM((head_dim, rows), jnp.float32),
    ]
    q_spec = pl.BlockSpec((tok_rows, qwidth), lambda h, rel: (0, h))

    state = None
    out = None
    for stage in range(reach + 1):
        first = stage == 0
        last = stage == reach
        kernel = make_stage(stage, first, last, dev_blocks, doc_blk, firsts, groups, head_dim, score_scale)
        kv_spec = pl.BlockSpec((k_src[stage].shape[0], head_dim), lambda h, rel: (0, h))
        in_specs = [q_spec, kv_spec, kv_spec] + ([] if first else state_specs)
        args = [rel_start, q2, k_src[stage], v_src[stage]] + ([] if first else list(state))
        if last:
            out_shape = jax.ShapeDtypeStruct((tok_rows, heads * qwidth), queries.dtype)
            out_specs = q_spec
        else:
            out_shape = state_shapes
            out_specs = state_specs
        res = pl.pallas_call(
            kernel,
            out_shape=out_shape,
            grid_spec=pltpu.PrefetchScalarGridSpec(
                num_scalar_prefetch=1,
                grid=(heads,),
                in_specs=in_specs,
                out_specs=out_specs,
                scratch_shapes=scratch,
            ),
            compiler_params=pltpu.CompilerParams(dimension_semantics=("arbitrary",)),
        )(*args)
        if last:
            out = res
        else:
            state = res
    return out.reshape(tok_rows, heads, qwidth)


def solution(mesh):
    placed = (
        P(("grp", "seq"), "head", None),
        P(("grp", "seq"), "head", None),
        P(("grp", "seq"), "head", None),
        P("grp"),
    )

    return jax.shard_map(
        on_device,
        mesh=mesh,
        in_specs=placed,
        out_specs=P(("grp", "seq"), "head", None),
        check_vma=False,
    )
```

profile of v0, /device:TPU:12, one launch (start us, length us, event | category | flops | bytes accessed | tf_op | source)
XLA Modules:
  0.0 49.2 jit_solution(4012668750697317688)
XLA Ops:
  0.0 1.0 %copy.11 = bf16[64,8,2,128]{3,1,2,0:T(8,128)(2,1)S(1)} copy(bf16[64,8,2,128]{3,2,1,0:T(2,128)(2,1)} %bitcast.21) | data formatting | bytes 524288
  1.0 0.0 copy-start
  1.0 3.5 %collective-permute-start = (bf16[512,256]{1,0:T(8,128)(2,1)S(1)}, bf16[512,256]{1,0:T(8,128)(2,1)S(1)}, u32[]{:S(2)}, u32[]{:S(2)}) collective-permute-start(bf16[512,256]{1,0:T(8,128)(2,1)S(1)} %bitcast.17), channel_id=1, source_target_pairs={{0,4},{4,8},{8,12},{1,5},{5,9},{9,13},{2,6},{6,10},{10,14},{3,7},{... | collective-permute-start | bytes 786440 | tf_op jit(solution)/shard_map/ppermute | solution.py:14
  4.5 1.0 %copy.10 = bf16[64,8,2,128]{3,1,2,0:T(8,128)(2,1)S(1)} copy(bf16[64,8,2,128]{3,2,1,0:T(2,128)(2,1)} %bitcast.22) | data formatting | bytes 524288
  5.5 0.0 copy-start.1
  5.5 3.5 %collective-permute-start.2 = (bf16[512,256]{1,0:T(8,128)(2,1)S(1)}, bf16[512,256]{1,0:T(8,128)(2,1)S(1)}, u32[]{:S(2)}, u32[]{:S(2)}) collective-permute-start(bf16[512,256]{1,0:T(8,128)(2,1)S(1)} %bitcast.19), channel_id=1, source_target_pairs={{0,4},{4,8},{8,12},{1,5},{5,9},{9,13},{2,6},{6,10},{10,14},{3,7},{... | collective-permute-start | bytes 786440 | tf_op jit(solution)/shard_map/ppermute | solution.py:14
  9.0 2.4 %copy.5 = bf16[64,8,2,512]{3,1,2,0:T(8,128)(2,1)} copy(bf16[64,8,2,512]{3,2,1,0:T(2,128)(2,1)} %bitcast.16) | data formatting | bytes 2097152
  11.5 0.0 copy-done.6
  11.5 0.2 reduce-window.9
  11.6 0.2 select_reduce_fusion
  11.8 0.3 collective-permute-done.k_ref
  12.1 3.5 %collective-permute-start.1 = (bf16[384,256]{1,0:T(8,128)(2,1)S(1)}, bf16[384,256]{1,0:T(8,128)(2,1)S(1)}, u32[]{:S(2)}, u32[]{:S(2)}) collective-permute-start(bf16[384,256]{1,0:T(8,128)(2,1)S(1)} %slice.8), channel_id=1, source_target_pairs={{0,4},{4,8},{8,12},{1,5},{5,9},{9,13},{2,6},{6,10},{10,14},{3,7},{... | collective-permute-start | bytes 589832 | tf_op jit(solution)/shard_map/ppermute | solution.py:14
  15.6 1.9 %collective-permute-done.2.v_ref = bf16[512,256]{1,0:T(8,128)(2,1)S(1)} collective-permute-done((bf16[512,256]{1,0:T(8,128)(2,1)S(1)}, bf16[512,256]{1,0:T(8,128)(2,1)S(1)}, u32[]{:S(2)}, u32[]{:S(2)}) %collective-permute-start.2) | collective-permute-done | bytes 262176 | tf_op jit(solution)/shard_map/ppermute | solution.py:14
  17.5 3.7 %collective-permute-start.3 = (bf16[384,256]{1,0:T(8,128)(2,1)S(1)}, bf16[384,256]{1,0:T(8,128)(2,1)S(1)}, u32[]{:S(2)}, u32[]{:S(2)}) collective-permute-start(bf16[384,256]{1,0:T(8,128)(2,1)S(1)} %slice.9), channel_id=1, source_target_pairs={{0,4},{4,8},{8,12},{1,5},{5,9},{9,13},{2,6},{6,10},{10,14},{3,7},{... | collective-permute-start | bytes 589832 | tf_op jit(solution)/shard_map/ppermute | solution.py:14
  21.2 0.6 %broadcast_subtract_fusion.rel_ref = s32[4]{0:T(128)} fusion(s32[4]{0:T(128)S(1)} %select_reduce_fusion, s32[]{:T(128)S(6)} %mul.3), kind=kLoop, calls=%fused_computation.5 | loop fusion | flops 4 | bytes 36 | tf_op jit(solution)/shard_map/sub | solution.py:162
  21.8 8.6 %shard_map.46 = (f32[2,4,128,512]{3,2,1,0:T(8,128)}, f32[2,4,512]{2,1,0:T(4,128)}, f32[2,4,512]{2,1,0:T(4,128)}) custom-call(s32[4]{0:T(128)} %broadcast_subtract_fusion.rel_ref, bf16[512,1024]{1,0:T(8,128)(2,1)} %bitcast.13, bf16[512,256]{1,0:T(8,128)(2,1)} %bitcast.18, bf16[512,256]{1,0:T(8,128)(2,1)} %bitcast.20), custom_call_target="tpu_custom_call" | custom-call | tf_op jit(solution)/shard_map/pallas_call | solution.py:211
  30.4 11.4 %shard_map.47 = (f32[2,4,128,512]{3,2,1,0:T(8,128)}, f32[2,4,512]{2,1,0:T(4,128)}, f32[2,4,512]{2,1,0:T(4,128)}) custom-call(s32[4]{0:T(128)} %broadcast_subtract_fusion.rel_ref, bf16[512,1024]{1,0:T(8,128)(2,1)} %bitcast.14, bf16[512,256]{1,0:T(8,128)(2,1)} %copy-done.2, bf16[512,256]{1,0:T(8,128)(2,1)} %copy-done.3, ...), custom_call_target="tpu_custom_call" | custom-call | tf_op jit(solution)/shard_map/pallas_call | solution.py:211
  41.8 0.0 collective-permute-done.1.k_ref
  41.8 0.0 collective-permute-done.3.v_ref
  41.8 0.0 copy-start.5
  41.8 0.7 %copy-done.4 = bf16[384,256]{1,0:T(8,128)(2,1)} copy-done((bf16[384,256]{1,0:T(8,128)(2,1)}, bf16[384,256]{1,0:T(8,128)(2,1)S(1)}, u32[]{:S(2)}) %copy-start.4) | copy-done | bytes 196632
  42.5 0.1 copy-done.5
  42.5 4.0 %shard_map.48 = bf16[512,1024]{1,0:T(8,128)(2,1)} custom-call(s32[4]{0:T(128)} %broadcast_subtract_fusion.rel_ref, bf16[512,1024]{1,0:T(8,128)(2,1)} %bitcast.15, bf16[384,256]{1,0:T(8,128)(2,1)} %copy-done.4, bf16[384,256]{1,0:T(8,128)(2,1)} %copy-done.5, f32[2,4,128,512]{3,2,1,0:T(8,128)} %get-tuple-element.14.refs_0_, ...), custom_call_target="tpu_custom_call" | custom-call | tf_op jit(solution)/shard_map/pallas_call | solution.py:211
  46.5 2.6 %reshape.48 = bf16[512,2,512]{2,1,0:T(2,128)(2,1)} reshape(bf16[512,1024]{1,0:T(8,128)(2,1)} %shard_map.48) | data formatting | bytes 2097152 | tf_op jit(solution)/shard_map/reshape | solution.py:227
  (11 shorter events, 0.0 us)
Async XLA Ops:
  0.0 11.5 %copy-start.6 = (s32[4]{0:T(128)S(1)}, s32[4]{0:T(128)}, u32[]{:S(2)}) copy-start(s32[4]{0:T(128)} %param.7) | copy-start | bytes 52
  1.0 20.8 %copy-start = (bf16[64,8,2,128]{3,1,2,0:T(8,128)(2,1)}, bf16[64,8,2,128]{3,1,2,0:T(8,128)(2,1)S(1)}, u32[]{:S(2)}) copy-start(bf16[64,8,2,128]{3,1,2,0:T(8,128)(2,1)S(1)} %copy.11) | copy-start | bytes 786436
  1.0 11.1 %collective-permute-start = (bf16[512,256]{1,0:T(8,128)(2,1)S(1)}, bf16[512,256]{1,0:T(8,128)(2,1)S(1)}, u32[]{:S(2)}, u32[]{:S(2)}) collective-permute-start(bf16[512,256]{1,0:T(8,128)(2,1)S(1)} %bitcast.17), channel_id=1, source_target_pairs={{0,4},{4,8},{8,12},{1,5},{5,9},{9,13},{2,6},{6,10},{10,14},{3,7},{... | collective-permute-start | bytes 786440 | tf_op jit(solution)/shard_map/ppermute | solution.py:14
  5.5 16.3 %copy-start.1 = (bf16[64,8,2,128]{3,1,2,0:T(8,128)(2,1)}, bf16[64,8,2,128]{3,1,2,0:T(8,128)(2,1)S(1)}, u32[]{:S(2)}) copy-start(bf16[64,8,2,128]{3,1,2,0:T(8,128)(2,1)S(1)} %copy.10) | copy-start | bytes 786436
  5.5 12.0 %collective-permute-start.2 = (bf16[512,256]{1,0:T(8,128)(2,1)S(1)}, bf16[512,256]{1,0:T(8,128)(2,1)S(1)}, u32[]{:S(2)}, u32[]{:S(2)}) collective-permute-start(bf16[512,256]{1,0:T(8,128)(2,1)S(1)} %bitcast.19), channel_id=1, source_target_pairs={{0,4},{4,8},{8,12},{1,5},{5,9},{9,13},{2,6},{6,10},{10,14},{3,7},{... | collective-permute-start | bytes 786440 | tf_op jit(solution)/shard_map/ppermute | solution.py:14
  12.1 18.3 %copy-start.2 = (bf16[512,256]{1,0:T(8,128)(2,1)}, bf16[512,256]{1,0:T(8,128)(2,1)S(1)}, u32[]{:S(2)}) copy-start(bf16[512,256]{1,0:T(8,128)(2,1)S(1)} %collective-permute-done.k_ref) | copy-start | bytes 786436
  12.1 29.7 %collective-permute-start.1 = (bf16[384,256]{1,0:T(8,128)(2,1)S(1)}, bf16[384,256]{1,0:T(8,128)(2,1)S(1)}, u32[]{:S(2)}, u32[]{:S(2)}) collective-permute-start(bf16[384,256]{1,0:T(8,128)(2,1)S(1)} %slice.8), channel_id=1, source_target_pairs={{0,4},{4,8},{8,12},{1,5},{5,9},{9,13},{2,6},{6,10},{10,14},{3,7},{... | collective-permute-start | bytes 589832 | tf_op jit(solution)/shard_map/ppermute | solution.py:14
  17.5 12.9 %copy-start.3 = (bf16[512,256]{1,0:T(8,128)(2,1)}, bf16[512,256]{1,0:T(8,128)(2,1)S(1)}, u32[]{:S(2)}) copy-start(bf16[512,256]{1,0:T(8,128)(2,1)S(1)} %collective-permute-done.2.v_ref) | copy-start | bytes 786436
  17.5 24.3 %collective-permute-start.3 = (bf16[384,256]{1,0:T(8,128)(2,1)S(1)}, bf16[384,256]{1,0:T(8,128)(2,1)S(1)}, u32[]{:S(2)}, u32[]{:S(2)}) collective-permute-start(bf16[384,256]{1,0:T(8,128)(2,1)S(1)} %slice.9), channel_id=1, source_target_pairs={{0,4},{4,8},{8,12},{1,5},{5,9},{9,13},{2,6},{6,10},{10,14},{3,7},{... | collective-permute-start | bytes 589832 | tf_op jit(solution)/shard_map/ppermute | solution.py:14
  41.8 0.7 %copy-start.4 = (bf16[384,256]{1,0:T(8,128)(2,1)}, bf16[384,256]{1,0:T(8,128)(2,1)S(1)}, u32[]{:S(2)}) copy-start(bf16[384,256]{1,0:T(8,128)(2,1)S(1)} %collective-permute-done.1.k_ref) | copy-start | bytes 589828
  41.8 0.7 %copy-start.5 = (bf16[384,256]{1,0:T(8,128)(2,1)}, bf16[384,256]{1,0:T(8,128)(2,1)S(1)}, u32[]{:S(2)}) copy-start(bf16[384,256]{1,0:T(8,128)(2,1)S(1)} %collective-permute-done.3.v_ref) | copy-start | bytes 589828
where the time goes:
time: 49.5 us; the launch traced here: 49.2 us
  Pallas kernels  23.9 us (48%)
  starting transfers between devices  14.1 us (28%)
  local copies, waits for them, and re-layouts  7.82 us (16%)
  waiting for transfers between devices  2.17 us (4%)
  other arithmetic  0.97 us (2%)
    pallas_call x3, Pallas kernels, on_device(): pl.pallas_call(kernel, out_shape=out_shape, grid_spec=pltpu.PrefetchScala...  23.9 us
    ppermute x4, starting transfers between devices, shift_up(): return lax.ppermute(block, axis, [(i, i + 1) for i in range(size - 1)])  14.1 us
    unnamed x17, local copies, waits for them, and re-layouts  5.17 us
    reshape x1, local copies, waits for them, and re-layouts, on_device(): return out.reshape(tok_rows, heads, qwidth)  2.62 us
    ppermute x4, waiting for transfers between devices, shift_up(): return lax.ppermute(block, axis, [(i, i + 1) for i in range(size - 1)])  2.17 us
  transfers between devices with their start and end apart: 4, of which 2 were waited for; matrix products, arithmetic and copies ran while one was open for 9% of the time, Pallas kernels for 41%

commit v1 on v0

--- a/solution.py
+++ b/solution.py
@@ -40,7 +40,9 @@
             return rel
         return rel + stage * dev_blocks - firsts[stage]
 
-    def kernel(rel_ref, q_ref, k_ref, v_ref, *refs):
+    def kernel(rel_ref, q_ref, kv_ref, *refs):
+        k_ref = kv_ref.at[0]
+        v_ref = kv_ref.at[1]
         if first:
             acc_in = m_in = l_in = None
             rest = refs
@@ -165,15 +167,14 @@
     k2 = keys.reshape(tok_rows, heads * head_dim)
     v2 = values.reshape(tok_rows, heads * head_dim)
 
-    k_src, v_src = [k2], [v2]
-    k_cur, v_cur = k2, v2
+    kv_cur = jnp.stack([k2, v2])
+    kv_src = [kv_cur]
     prev_first = 0
     for r in range(1, reach + 1):
         cut = (firsts[r] - prev_first) * BLK
-        k_cur, v_cur = shift_up((k_cur[cut:], v_cur[cut:]), "seq")
+        kv_cur = shift_up(kv_cur[:, cut:], "seq")
         prev_first = firsts[r]
-        k_src.append(k_cur)
-        v_src.append(v_cur)
+        kv_src.append(kv_cur)
 
     state_shapes = (
         jax.ShapeDtypeStruct((heads, dev_blocks, head_dim, rows), jnp.float32),
@@ -199,9 +200,9 @@
         first = stage == 0
         last = stage == reach
         kernel = make_stage(stage, first, last, dev_blocks, doc_blk, firsts, groups, head_dim, score_scale)
-        kv_spec = pl.BlockSpec((k_src[stage].shape[0], head_dim), lambda h, rel: (0, h))
-        in_specs = [q_spec, kv_spec, kv_spec] + ([] if first else state_specs)
-        args = [rel_start, q2, k_src[stage], v_src[stage]] + ([] if first else list(state))
+        kv_spec = pl.BlockSpec((2, kv_src[stage].shape[1], head_dim), lambda h, rel: (0, 0, h))
+        in_specs = [q_spec, kv_spec] + ([] if first else state_specs)
+        args = [rel_start, q2, kv_src[stage]] + ([] if first else list(state))
         if last:
             out_shape = jax.ShapeDtypeStruct((tok_rows, heads * qwidth), queries.dtype)
             out_specs = q_spec

time: 49.5 us -> 51.2 us (1.034)
  waiting for transfers between devices: 2.17 us -> 11.9 us
  starting transfers between devices: 14.1 us -> 6.97 us
  local copies, waits for them, and re-layouts: 7.82 us -> 6.99 us
    ppermute x4 -> x2, waiting for transfers between devices: 2.17 us -> 11.9 us  [shift_up(): return lax.ppermute(block, axis, [(i, i + 1) for i in range(size - 1)])]
    ppermute x4 -> x2, starting transfers between devices: 14.1 us -> 6.97 us  [shift_up(): return lax.ppermute(block, axis, [(i, i + 1) for i in range(size - 1)])]
    unnamed x17 -> x12, local copies, waits for them, and re-layouts: 5.17 us -> 1.99 us
    another operation x0 -> x3, local copies, waits for them, and re-layouts: none -> 2.35 us  [on_device(): kv_cur = jnp.stack([k2, v2])]
  transfers between devices with their start and end apart: 4 -> 2, of which waited for: 2 -> 1; matrix products, arithmetic and copies ran while one was open for 9% -> 4% of each run, Pallas kernels for 41% -> 39%
where the time goes in v1:
time: 51.2 us; the launch traced here: 50.9 us
  Pallas kernels  24 us (47%)
  waiting for transfers between devices  11.9 us (23%)
  local copies, waits for them, and re-layouts  6.99 us (14%)
  starting transfers between devices  6.97 us (14%)
  other arithmetic  0.96 us (2%)
    pallas_call x3, Pallas kernels, on_device(): pl.pallas_call(kernel, out_shape=out_shape, grid_spec=pltpu.PrefetchScala...  24 us
    ppermute x2, waiting for transfers between devices, shift_up(): return lax.ppermute(block, axis, [(i, i + 1) for i in range(size - 1)])  11.9 us
    ppermute x2, starting transfers between devices, shift_up(): return lax.ppermute(block, axis, [(i, i + 1) for i in range(size - 1)])  6.97 us
    reshape x1, local copies, waits for them, and re-layouts, on_device(): return out.reshape(tok_rows, heads, qwidth)  2.62 us
    another operation x3, local copies, waits for them, and re-layouts, on_device(): kv_cur = jnp.stack([k2, v2])  2.35 us
    unnamed x12, local copies, waits for them, and re-layouts  1.99 us
  transfers between devices with their start and end apart: 2, of which 1 were waited for; matrix products, arithmetic and copies ran while one was open for 4% of the time, Pallas kernels for 39%

profile of v1, /device:TPU:12, one launch (start us, length us, event | category | flops | bytes accessed | tf_op | source)
XLA Modules:
  0.0 50.9 jit_solution(4130590200590756218)
XLA Ops:
  0.0 0.0 copy-start.4
  0.0 0.0 copy-start.2
  0.0 1.2 %stack_reshape.6 = bf16[1,512,256]{2,1,0:T(8,128)(2,1)S(1)} reshape(bf16[512,2,128]{2,1,0:T(2,128)(2,1)} %param.5) | data formatting | bytes 524288 | tf_op jit(solution)/shard_map/stack;reshape | solution.py:170
  1.2 1.1 %stack_reshape.7 = bf16[1,512,256]{2,1,0:T(8,128)(2,1)S(1)} reshape(bf16[512,2,128]{2,1,0:T(2,128)(2,1)} %param.6) | data formatting | bytes 524288 | tf_op jit(solution)/shard_map/stack;reshape | solution.py:170
  2.4 0.0 copy-start.1
  2.4 3.5 %collective-permute-start = (bf16[2,512,256]{2,1,0:T(8,128)(2,1)S(1)}, bf16[2,512,256]{2,1,0:T(8,128)(2,1)S(1)}, u32[]{:S(2)}, u32[]{:S(2)}) collective-permute-start(bf16[2,512,256]{2,1,0:T(8,128)(2,1)S(1)} %constant_dynamic-update-slice_fusion.kv_ref), channel_id=1, source_target_pairs={{0,4},{4,8},{8,12},{1,5},{5,9},{9,13},{2,6},{6,10},{10,14},{3,7},{... | collective-permute-start | bytes 1572872 | tf_op jit(solution)/shard_map/ppermute | solution.py:14
  5.9 0.0 copy-done.4
  5.9 0.2 reduce-window.9
  6.1 11.9 %collective-permute-done.kv_ref = bf16[2,512,256]{2,1,0:T(8,128)(2,1)S(1)} collective-permute-done((bf16[2,512,256]{2,1,0:T(8,128)(2,1)S(1)}, bf16[2,512,256]{2,1,0:T(8,128)(2,1)S(1)}, u32[]{:S(2)}, u32[]{:S(2)}) %collective-permute-start) | collective-permute-done | bytes 524320 | tf_op jit(solution)/shard_map/ppermute | solution.py:14
  18.0 0.0 copy-start
  18.0 3.5 %collective-permute-start.1 = (bf16[2,384,256]{2,1,0:T(8,128)(2,1)S(1)}, bf16[2,384,256]{2,1,0:T(8,128)(2,1)S(1)}, u32[]{:S(2)}, u32[]{:S(2)}) collective-permute-start(bf16[2,384,256]{2,1,0:T(8,128)(2,1)S(1)} %slice.4), channel_id=1, source_target_pairs={{0,4},{4,8},{8,12},{1,5},{5,9},{9,13},{2,6},{6,10},{10,14},{3,7},{... | collective-permute-start | bytes 1179656 | tf_op jit(solution)/shard_map/ppermute | solution.py:14
  21.5 0.0 copy-done.2
  21.5 1.2 %copy.5 = bf16[64,8,2,512]{3,1,2,0:T(8,128)(2,1)} copy(bf16[64,8,2,512]{3,2,1,0:T(2,128)(2,1)S(1)} %bitcast.8) | data formatting | bytes 2097152
  22.7 0.2 select_reduce_fusion
  22.9 0.6 %broadcast_subtract_fusion.rel_ref = s32[4]{0:T(128)} fusion(s32[4]{0:T(128)S(1)} %select_reduce_fusion, s32[]{:T(128)S(6)} %mul.3), kind=kLoop, calls=%fused_computation.5 | loop fusion | flops 4 | bytes 36 | tf_op jit(solution)/shard_map/sub | solution.py:164
  23.5 0.0 copy-done.1
  23.5 8.5 %shard_map.46 = (f32[2,4,128,512]{3,2,1,0:T(8,128)}, f32[2,4,512]{2,1,0:T(4,128)}, f32[2,4,512]{2,1,0:T(4,128)}) custom-call(s32[4]{0:T(128)} %broadcast_subtract_fusion.rel_ref, bf16[512,1024]{1,0:T(8,128)(2,1)} %bitcast.5, bf16[2,512,256]{2,1,0:T(8,128)(2,1)} %copy-done.1), custom_call_target="tpu_custom_call" | custom-call | tf_op jit(solution)/shard_map/pallas_call | solution.py:212
  32.1 0.0 copy-done
  32.1 11.4 %shard_map.47 = (f32[2,4,128,512]{3,2,1,0:T(8,128)}, f32[2,4,512]{2,1,0:T(4,128)}, f32[2,4,512]{2,1,0:T(4,128)}) custom-call(s32[4]{0:T(128)} %broadcast_subtract_fusion.rel_ref, bf16[512,1024]{1,0:T(8,128)(2,1)} %bitcast.6, bf16[2,512,256]{2,1,0:T(8,128)(2,1)} %copy-done, f32[2,4,128,512]{3,2,1,0:T(8,128)} %get-tuple-element.11.refs_0_, ...), custom_call_target="tpu_custom_call" | custom-call | tf_op jit(solution)/shard_map/pallas_call | solution.py:212
  43.4 0.0 collective-permute-done.1.kv_ref
  43.4 0.0 copy-start.3
  43.4 0.7 %copy-done.3 = bf16[2,384,256]{2,1,0:T(8,128)(2,1)} copy-done((bf16[2,384,256]{2,1,0:T(8,128)(2,1)}, bf16[2,384,256]{2,1,0:T(8,128)(2,1)S(1)}, u32[]{:S(2)}) %copy-start.3) | copy-done | bytes 393240
  44.2 4.1 %shard_map.48 = bf16[512,1024]{1,0:T(8,128)(2,1)} custom-call(s32[4]{0:T(128)} %broadcast_subtract_fusion.rel_ref, bf16[512,1024]{1,0:T(8,128)(2,1)} %bitcast.7, bf16[2,384,256]{2,1,0:T(8,128)(2,1)} %copy-done.3, f32[2,4,128,512]{3,2,1,0:T(8,128)} %get-tuple-element.14.refs_0_, f32[2,4,512]{2,1,0:T(4,128)} %get-tuple-element.15.refs_1_, ...), custom_call_target="tpu_custom_call" | custom-call | tf_op jit(solution)/shard_map/pallas_call | solution.py:212
  48.3 2.6 %reshape.40 = bf16[512,2,512]{2,1,0:T(2,128)(2,1)} reshape(bf16[512,1024]{1,0:T(8,128)(2,1)} %shard_map.48) | data formatting | bytes 2097152 | tf_op jit(solution)/shard_map/reshape | solution.py:228
  (4 shorter events, 0.1 us)
Async XLA Ops:
  0.0 5.9 %copy-start.4 = (s32[4]{0:T(128)S(1)}, s32[4]{0:T(128)}, u32[]{:S(2)}) copy-start(s32[4]{0:T(128)} %param.7) | copy-start | bytes 52
  0.0 21.5 %copy-start.2 = (bf16[512,2,512]{2,1,0:T(2,128)(2,1)S(1)}, bf16[512,2,512]{2,1,0:T(2,128)(2,1)}, u32[]{:S(2)}) copy-start(bf16[512,2,512]{2,1,0:T(2,128)(2,1)} %param.4) | copy-start | bytes 3145732
  2.4 21.1 %copy-start.1 = (bf16[2,512,256]{2,1,0:T(8,128)(2,1)}, bf16[2,512,256]{2,1,0:T(8,128)(2,1)S(1)}, u32[]{:S(2)}) copy-start(bf16[2,512,256]{2,1,0:T(8,128)(2,1)S(1)} %constant_dynamic-update-slice_fusion.kv_ref) | copy-start | bytes 1572868
  2.4 15.6 %collective-permute-start = (bf16[2,512,256]{2,1,0:T(8,128)(2,1)S(1)}, bf16[2,512,256]{2,1,0:T(8,128)(2,1)S(1)}, u32[]{:S(2)}, u32[]{:S(2)}) collective-permute-start(bf16[2,512,256]{2,1,0:T(8,128)(2,1)S(1)} %constant_dynamic-update-slice_fusion.kv_ref), channel_id=1, source_target_pairs={{0,4},{4,8},{8,12},{1,5},{5,9},{9,13},{2,6},{6,10},{10,14},{3,7},{... | collective-permute-start | bytes 1572872 | tf_op jit(solution)/shard_map/ppermute | solution.py:14
  18.0 14.1 %copy-start = (bf16[2,512,256]{2,1,0:T(8,128)(2,1)}, bf16[2,512,256]{2,1,0:T(8,128)(2,1)S(1)}, u32[]{:S(2)}) copy-start(bf16[2,512,256]{2,1,0:T(8,128)(2,1)S(1)} %collective-permute-done.kv_ref) | copy-start | bytes 1572868
  18.0 25.4 %collective-permute-start.1 = (bf16[2,384,256]{2,1,0:T(8,128)(2,1)S(1)}, bf16[2,384,256]{2,1,0:T(8,128)(2,1)S(1)}, u32[]{:S(2)}, u32[]{:S(2)}) collective-permute-start(bf16[2,384,256]{2,1,0:T(8,128)(2,1)S(1)} %slice.4), channel_id=1, source_target_pairs={{0,4},{4,8},{8,12},{1,5},{5,9},{9,13},{2,6},{6,10},{10,14},{3,7},{... | collective-permute-start | bytes 1179656 | tf_op jit(solution)/shard_map/ppermute | solution.py:14
  43.4 0.7 %copy-start.3 = (bf16[2,384,256]{2,1,0:T(8,128)(2,1)}, bf16[2,384,256]{2,1,0:T(8,128)(2,1)S(1)}, u32[]{:S(2)}) copy-start(bf16[2,384,256]{2,1,0:T(8,128)(2,1)S(1)} %collective-permute-done.1.kv_ref) | copy-start | bytes 1179652

commit v2 on v1

--- a/solution.py
+++ b/solution.py
@@ -51,92 +51,83 @@
             rest = refs[3:]
         if last:
             o_ref = rest[0]
-            s_sc, m_sc, l_sc, acc_sc = rest[1:]
+            (s_sc,) = rest[1:]
         else:
             acc_out, m_out, l_out = rest[:3]
-            s_sc, m_sc, l_sc, acc_sc = rest[3:]
+            (s_sc,) = rest[3:]
 
         for i in range(dev_blocks):
             start = rel_ref[i]
             regions = stage_regions(stage, i, dev_blocks, doc_blk, firsts)
-            if first:
-                m_old = jnp.full((1, groups * BLK), -jnp.inf, jnp.float32)
-                l_old = jnp.zeros((1, groups * BLK), jnp.float32)
-            else:
-                m_old = m_in[i : i + 1, :]
-                l_old = l_in[i : i + 1, :]
-            m_sc[...] = m_old
+
+            def finish(m_new, row_sum, acc):
+                if last:
+                    out = jnp.transpose(acc * (1.0 / row_sum))
+                    for g in range(groups):
+                        o_ref[i * BLK : (i + 1) * BLK, g * head_dim : (g + 1) * head_dim] = out[
+                            g * BLK : (g + 1) * BLK
+                        ].astype(o_ref.dtype)
+                else:
+                    acc_out[i] = acc
+                    m_out[i : i + 1, :] = m_new
+                    l_out[i : i + 1, :] = row_sum
+
+            def passthrough():
+                finish(m_in[i : i + 1, :], l_in[i : i + 1, :], acc_in[i])
+
             if not regions:
-                m_new = m_old
-                l_sc[...] = l_old
-                if first:
-                    acc_sc[...] = jnp.zeros(acc_sc.shape, jnp.float32)
-                else:
-                    acc_sc[...] = acc_in[i]
-            else:
+                passthrough()
+                continue
+
+            def compute():
                 q = jnp.concatenate(
                     [q_ref[i * BLK : (i + 1) * BLK, g * head_dim : (g + 1) * head_dim] for g in range(groups)],
                     axis=0,
                 )
-
-                def scores(rels):
+                m_blk = None
+                for r, rels in enumerate(regions):
                     lo = local_index(rels[0])
                     k = k_ref[lo * BLK : (lo + len(rels)) * BLK, :]
-                    s = lax.dot_general(
+                    sc = lax.dot_general(
                         k, q, (((1,), (1,)), ((), ())), preferred_element_type=jnp.float32
                     ) * score_scale
+                    key = lax.broadcasted_iota(jnp.int32, sc.shape, 0) // BLK + rels[0]
+                    keep = key >= start
                     if rels[-1] == i:
-                        key = lax.broadcasted_iota(jnp.int32, s.shape, 0) + (rels[0] - i) * BLK
-                        tok = lax.broadcasted_iota(jnp.int32, s.shape, 1) % BLK
-                        s = jnp.where(key <= tok, s, -jnp.inf)
-                    return s
-
-                def variants(rels):
-                    out = [(rels, start <= rels[0])]
-                    if len(rels) == 2:
-                        out.append((rels[1:], start == rels[1]))
-                    return out
-
+                        key_pos = lax.broadcasted_iota(jnp.int32, sc.shape, 0) + (rels[0] - i) * BLK
+                        tok = lax.broadcasted_iota(jnp.int32, sc.shape, 1) % BLK
+                        keep = keep & (key_pos <= tok)
+                    sc = jnp.where(keep, sc, -jnp.inf)
+                    s_sc[r, : len(rels) * BLK, :] = sc
+                    mx = jnp.max(sc, axis=0, keepdims=True)
+                    m_blk = mx if m_blk is None else jnp.maximum(m_blk, mx)
+                if first:
+                    m_new = m_blk
+                    row_sum = jnp.zeros(m_new.shape, jnp.float32)
+                    acc = jnp.zeros((head_dim, groups * BLK), jnp.float32)
+                else:
+                    m_old = m_in[i : i + 1, :]
+                    m_new = jnp.maximum(m_old, m_blk)
+                    alpha = jnp.exp(m_old - m_new)
+                    row_sum = alpha * l_in[i : i + 1, :]
+                    acc = alpha * acc_in[i]
                 for r, rels in enumerate(regions):
-                    for sub, cond in variants(rels):
-                        @pl.when(cond)
-                        def _():
-                            s = scores(sub)
-                            s_sc[r, : len(sub) * BLK, :] = s
-                            m_sc[...] = jnp.maximum(m_sc[...], jnp.max(s, axis=0, keepdims=True))
-
-                m_new = m_sc[...]
-                alpha = jnp.exp(m_old - m_new)
-                l_sc[...] = alpha * l_old
-                if first:
-                    acc_sc[...] = jnp.zeros(acc_sc.shape, jnp.float32)
-                else:
-                    acc_sc[...] = alpha * acc_in[i]
-
-                for r, rels in enumerate(regions):
-                    for sub, cond in variants(rels):
-                        @pl.when(cond)
-                        def _():
-                            p = jnp.exp(s_sc[r, : len(sub) * BLK, :] - m_new)
-                            l_sc[...] = l_sc[...] + jnp.sum(p, axis=0, keepdims=True)
-                            lo = local_index(sub[0])
-                            v = v_ref[lo * BLK : (lo + len(sub)) * BLK, :]
-                            acc_sc[...] = acc_sc[...] + lax.dot_general(
-                                v, p.astype(jnp.bfloat16), (((0,), (0,)), ((), ())),
-                                preferred_element_type=jnp.float32,
-                            )
-
-            if last:
-                out_t = acc_sc[...] / l_sc[...]
-                out = jnp.transpose(out_t)
-                for g in range(groups):
-                    o_ref[i * BLK : (i + 1) * BLK, g * head_dim : (g + 1) * head_dim] = out[
-                        g * BLK : (g + 1) * BLK
-                    ].astype(o_ref.dtype)
+                    p = jnp.exp(s_sc[r, : len(rels) * BLK, :] - m_new)
+                    row_sum = row_sum + jnp.sum(p, axis=0, keepdims=True)
+                    lo = local_index(rels[0])
+                    v = v_ref[lo * BLK : (lo + len(rels)) * BLK, :]
+                    acc = acc + lax.dot_general(
+                        v, p.astype(jnp.bfloat16), (((0,), (0,)), ((), ())),
+                        preferred_element_type=jnp.float32,
+                    )
+                finish(m_new, row_sum, acc)
+
+            if first:
+                compute()
             else:
-                acc_out[i] = acc_sc[...]
-                m_out[i : i + 1, :] = m_new if regions else m_old
-                l_out[i : i + 1, :] = l_sc[...]
+                live = start <= regions[-1][-1]
+                pl.when(live)(compute)
+                pl.when(jnp.logical_not(live))(passthrough)
 
     return kernel
 
@@ -188,9 +179,6 @@
     ]
     scratch = [
         pltpu.VMEM((max(1, (dev_blocks + 1) // 2), 2 * BLK, rows), jnp.float32),
-        pltpu.VMEM((1, rows), jnp.float32),
-        pltpu.VMEM((1, rows), jnp.float32),
-        pltpu.VMEM((head_dim, rows), jnp.float32),
     ]
     q_spec = pl.BlockSpec((tok_rows, qwidth), lambda h, rel: (0, h))
 

time: 51.2 us -> 46 us (0.90)
  the two profiles are of different devices: /device:TPU:12 before, /device:TPU:14 now
where the time goes in v2:
time: 46 us; the launch traced here: 45.8 us
  Pallas kernels  18.9 us (41%)
  waiting for transfers between devices  11.9 us (26%)
  local copies, waits for them, and re-layouts  6.99 us (15%)
  starting transfers between devices  6.97 us (15%)
  other arithmetic  0.96 us (2%)
    pallas_call x3, Pallas kernels, on_device(): pl.pallas_call(kernel, out_shape=out_shape, grid_spec=pltpu.PrefetchScala...  18.9 us
    ppermute x2, waiting for transfers between devices, shift_up(): return lax.ppermute(block, axis, [(i, i + 1) for i in range(size - 1)])  11.9 us
    ppermute x2, starting transfers between devices, shift_up(): return lax.ppermute(block, axis, [(i, i + 1) for i in range(size - 1)])  6.97 us
    reshape x1, local copies, waits for them, and re-layouts, on_device(): return out.reshape(tok_rows, heads, qwidth)  2.62 us
    another operation x3, local copies, waits for them, and re-layouts, on_device(): kv_cur = jnp.stack([k2, v2])  2.35 us
    unnamed x12, local copies, waits for them, and re-layouts  1.99 us
  transfers between devices with their start and end apart: 2, of which 1 were waited for; matrix products, arithmetic and copies ran while one was open for 5% of the time, Pallas kernels for 32%

profile of v2, /device:TPU:14, one launch (start us, length us, event | category | flops | bytes accessed | tf_op | source)
XLA Modules:
  0.0 45.8 jit_solution(5655082801859370625)
XLA Ops:
  0.0 0.0 copy-start.4
  0.0 0.0 copy-start.2
  0.0 1.2 %stack_reshape.6 = bf16[1,512,256]{2,1,0:T(8,128)(2,1)S(1)} reshape(bf16[512,2,128]{2,1,0:T(2,128)(2,1)} %param.5) | data formatting | bytes 524288 | tf_op jit(solution)/shard_map/stack;reshape | solution.py:161
  1.2 1.1 %stack_reshape.7 = bf16[1,512,256]{2,1,0:T(8,128)(2,1)S(1)} reshape(bf16[512,2,128]{2,1,0:T(2,128)(2,1)} %param.6) | data formatting | bytes 524288 | tf_op jit(solution)/shard_map/stack;reshape | solution.py:161
  2.4 0.0 copy-start.1
  2.4 3.5 %collective-permute-start = (bf16[2,512,256]{2,1,0:T(8,128)(2,1)S(1)}, bf16[2,512,256]{2,1,0:T(8,128)(2,1)S(1)}, u32[]{:S(2)}, u32[]{:S(2)}) collective-permute-start(bf16[2,512,256]{2,1,0:T(8,128)(2,1)S(1)} %constant_dynamic-update-slice_fusion.kv_ref), channel_id=1, source_target_pairs={{0,4},{4,8},{8,12},{1,5},{5,9},{9,13},{2,6},{6,10},{10,14},{3,7},{... | collective-permute-start | bytes 1572872 | tf_op jit(solution)/shard_map/ppermute | solution.py:14
  5.9 0.0 copy-done.4
  5.9 0.2 reduce-window.9
  6.1 11.9 %collective-permute-done.kv_ref = bf16[2,512,256]{2,1,0:T(8,128)(2,1)S(1)} collective-permute-done((bf16[2,512,256]{2,1,0:T(8,128)(2,1)S(1)}, bf16[2,512,256]{2,1,0:T(8,128)(2,1)S(1)}, u32[]{:S(2)}, u32[]{:S(2)}) %collective-permute-start) | collective-permute-done | bytes 524320 | tf_op jit(solution)/shard_map/ppermute | solution.py:14
  18.0 0.0 copy-start
  18.0 3.5 %collective-permute-start.1 = (bf16[2,384,256]{2,1,0:T(8,128)(2,1)S(1)}, bf16[2,384,256]{2,1,0:T(8,128)(2,1)S(1)}, u32[]{:S(2)}, u32[]{:S(2)}) collective-permute-start(bf16[2,384,256]{2,1,0:T(8,128)(2,1)S(1)} %slice.4), channel_id=1, source_target_pairs={{0,4},{4,8},{8,12},{1,5},{5,9},{9,13},{2,6},{6,10},{10,14},{3,7},{... | collective-permute-start | bytes 1179656 | tf_op jit(solution)/shard_map/ppermute | solution.py:14
  21.5 0.0 copy-done.2
  21.5 1.2 %copy.5 = bf16[64,8,2,512]{3,1,2,0:T(8,128)(2,1)} copy(bf16[64,8,2,512]{3,2,1,0:T(2,128)(2,1)S(1)} %bitcast.8) | data formatting | bytes 2097152
  22.7 0.2 select_reduce_fusion
  22.9 0.6 %broadcast_subtract_fusion.rel_ref = s32[4]{0:T(128)} fusion(s32[4]{0:T(128)S(1)} %select_reduce_fusion, s32[]{:T(128)S(6)} %mul.3), kind=kLoop, calls=%fused_computation.5 | loop fusion | flops 4 | bytes 36 | tf_op jit(solution)/shard_map/sub | solution.py:155
  23.5 0.0 copy-done.1
  23.5 6.3 %shard_map.46 = (f32[2,4,128,512]{3,2,1,0:T(8,128)}, f32[2,4,512]{2,1,0:T(4,128)}, f32[2,4,512]{2,1,0:T(4,128)}) custom-call(s32[4]{0:T(128)} %broadcast_subtract_fusion.rel_ref, bf16[512,1024]{1,0:T(8,128)(2,1)} %bitcast.5, bf16[2,512,256]{2,1,0:T(8,128)(2,1)} %copy-done.1), custom_call_target="tpu_custom_call" | custom-call | tf_op jit(solution)/shard_map/pallas_call | solution.py:200
  29.8 0.0 copy-done
  29.8 8.5 %shard_map.47 = (f32[2,4,128,512]{3,2,1,0:T(8,128)}, f32[2,4,512]{2,1,0:T(4,128)}, f32[2,4,512]{2,1,0:T(4,128)}) custom-call(s32[4]{0:T(128)} %broadcast_subtract_fusion.rel_ref, bf16[512,1024]{1,0:T(8,128)(2,1)} %bitcast.6, bf16[2,512,256]{2,1,0:T(8,128)(2,1)} %copy-done, f32[2,4,128,512]{3,2,1,0:T(8,128)} %get-tuple-element.11.refs_0_, ...), custom_call_target="tpu_custom_call" | custom-call | tf_op jit(solution)/shard_map/pallas_call | solution.py:200
  38.3 0.0 collective-permute-done.1.kv_ref
  38.3 0.0 copy-start.3
  38.3 0.7 %copy-done.3 = bf16[2,384,256]{2,1,0:T(8,128)(2,1)} copy-done((bf16[2,384,256]{2,1,0:T(8,128)(2,1)}, bf16[2,384,256]{2,1,0:T(8,128)(2,1)S(1)}, u32[]{:S(2)}) %copy-start.3) | copy-done | bytes 393240
  39.1 4.1 %shard_map.48 = bf16[512,1024]{1,0:T(8,128)(2,1)} custom-call(s32[4]{0:T(128)} %broadcast_subtract_fusion.rel_ref, bf16[512,1024]{1,0:T(8,128)(2,1)} %bitcast.7, bf16[2,384,256]{2,1,0:T(8,128)(2,1)} %copy-done.3, f32[2,4,128,512]{3,2,1,0:T(8,128)} %get-tuple-element.14.refs_0_, f32[2,4,512]{2,1,0:T(4,128)} %get-tuple-element.15.refs_1_, ...), custom_call_target="tpu_custom_call" | custom-call | tf_op jit(solution)/shard_map/pallas_call | solution.py:200
  43.1 2.6 %reshape.40 = bf16[512,2,512]{2,1,0:T(2,128)(2,1)} reshape(bf16[512,1024]{1,0:T(8,128)(2,1)} %shard_map.48) | data formatting | bytes 2097152 | tf_op jit(solution)/shard_map/reshape | solution.py:216
  (4 shorter events, 0.1 us)
Async XLA Ops:
  0.0 5.9 %copy-start.4 = (s32[4]{0:T(128)S(1)}, s32[4]{0:T(128)}, u32[]{:S(2)}) copy-start(s32[4]{0:T(128)} %param.7) | copy-start | bytes 52
  0.0 21.5 %copy-start.2 = (bf16[512,2,512]{2,1,0:T(2,128)(2,1)S(1)}, bf16[512,2,512]{2,1,0:T(2,128)(2,1)}, u32[]{:S(2)}) copy-start(bf16[512,2,512]{2,1,0:T(2,128)(2,1)} %param.4) | copy-start | bytes 3145732
  2.4 21.1 %copy-start.1 = (bf16[2,512,256]{2,1,0:T(8,128)(2,1)}, bf16[2,512,256]{2,1,0:T(8,128)(2,1)S(1)}, u32[]{:S(2)}) copy-start(bf16[2,512,256]{2,1,0:T(8,128)(2,1)S(1)} %constant_dynamic-update-slice_fusion.kv_ref) | copy-start | bytes 1572868
  2.4 15.6 %collective-permute-start = (bf16[2,512,256]{2,1,0:T(8,128)(2,1)S(1)}, bf16[2,512,256]{2,1,0:T(8,128)(2,1)S(1)}, u32[]{:S(2)}, u32[]{:S(2)}) collective-permute-start(bf16[2,512,256]{2,1,0:T(8,128)(2,1)S(1)} %constant_dynamic-update-slice_fusion.kv_ref), channel_id=1, source_target_pairs={{0,4},{4,8},{8,12},{1,5},{5,9},{9,13},{2,6},{6,10},{10,14},{3,7},{... | collective-permute-start | bytes 1572872 | tf_op jit(solution)/shard_map/ppermute | solution.py:14
  18.0 11.9 %copy-start = (bf16[2,512,256]{2,1,0:T(8,128)(2,1)}, bf16[2,512,256]{2,1,0:T(8,128)(2,1)S(1)}, u32[]{:S(2)}) copy-start(bf16[2,512,256]{2,1,0:T(8,128)(2,1)S(1)} %collective-permute-done.kv_ref) | copy-start | bytes 1572868
  18.0 20.3 %collective-permute-start.1 = (bf16[2,384,256]{2,1,0:T(8,128)(2,1)S(1)}, bf16[2,384,256]{2,1,0:T(8,128)(2,1)S(1)}, u32[]{:S(2)}, u32[]{:S(2)}) collective-permute-start(bf16[2,384,256]{2,1,0:T(8,128)(2,1)S(1)} %slice.4), channel_id=1, source_target_pairs={{0,4},{4,8},{8,12},{1,5},{5,9},{9,13},{2,6},{6,10},{10,14},{3,7},{... | collective-permute-start | bytes 1179656 | tf_op jit(solution)/shard_map/ppermute | solution.py:14
  38.3 0.7 %copy-start.3 = (bf16[2,384,256]{2,1,0:T(8,128)(2,1)}, bf16[2,384,256]{2,1,0:T(8,128)(2,1)S(1)}, u32[]{:S(2)}) copy-start(bf16[2,384,256]{2,1,0:T(8,128)(2,1)S(1)} %collective-permute-done.1.kv_ref) | copy-start | bytes 1179652

commit v3 on v2

--- a/solution.py
+++ b/solution.py
@@ -158,14 +158,14 @@
     k2 = keys.reshape(tok_rows, heads * head_dim)
     v2 = values.reshape(tok_rows, heads * head_dim)
 
-    kv_cur = jnp.stack([k2, v2])
-    kv_src = [kv_cur]
+    kv_cur = jnp.stack([keys, values])
+    kv_src = [jnp.stack([k2, v2])]
     prev_first = 0
     for r in range(1, reach + 1):
         cut = (firsts[r] - prev_first) * BLK
         kv_cur = shift_up(kv_cur[:, cut:], "seq")
         prev_first = firsts[r]
-        kv_src.append(kv_cur)
+        kv_src.append(kv_cur.reshape(2, kv_cur.shape[1], heads * head_dim))
 
     state_shapes = (
         jax.ShapeDtypeStruct((heads, dev_blocks, head_dim, rows), jnp.float32),

time: 46 us -> 49.3 us (1.072)
  the two profiles are of different devices: /device:TPU:14 before, /device:TPU:8 now
where the time goes in v3:
time: 49.3 us; the launch traced here: 48.9 us
  Pallas kernels  18.8 us (38%)
  waiting for transfers between devices  10.6 us (22%)
  local copies, waits for them, and re-layouts  7.54 us (15%)
  starting transfers between devices  6.97 us (14%)
  other arithmetic  4.95 us (10%)
    pallas_call x3, Pallas kernels, on_device(): pl.pallas_call(kernel, out_shape=out_shape, grid_spec=pltpu.PrefetchScala...  18.8 us
    ppermute x2, waiting for transfers between devices, shift_up(): return lax.ppermute(block, axis, [(i, i + 1) for i in range(size - 1)])  10.6 us
    ppermute x2, starting transfers between devices, shift_up(): return lax.ppermute(block, axis, [(i, i + 1) for i in range(size - 1)])  6.97 us
    reshape x1, local copies, waits for them, and re-layouts, on_device(): return out.reshape(tok_rows, heads, qwidth)  2.62 us
    reshape x2, local copies, waits for them, and re-layouts, on_device(): kv_src.append(kv_cur.reshape(2, kv_cur.shape[1], heads * head_dim))  2.13 us
    another operation x1, other arithmetic, on_device(): kv_cur = jnp.stack([keys, values])  1.91 us
    another operation x2, local copies, waits for them, and re-layouts, on_device(): kv_src = [jnp.stack([k2, v2])]  1.29 us
    unnamed x5, local copies, waits for them, and re-layouts  1.23 us
  transfers between devices with their start and end apart: 2, of which 1 were waited for; matrix products, arithmetic and copies ran while one was open for 14% of the time, Pallas kernels for 30%

profile of v3, /device:TPU:8, one launch (start us, length us, event | category | flops | bytes accessed | tf_op | source)
XLA Modules:
  0.0 48.9 jit_solution(1876434231344315937)
XLA Ops:
  0.0 0.0 copy-start.1
  0.0 0.0 copy-start
  0.0 1.9 %pad_maximum_fusion = bf16[2,512,2,128]{3,2,1,0:T(2,128)(2,1)S(1)} fusion(bf16[1,512,2,128]{3,2,1,0:T(2,128)(2,1)} %bitcast.12, bf16[1,512,2,128]{3,2,1,0:T(2,128)(2,1)} %bitcast.11), kind=kLoop, calls=%fused_computation | loop fusion | flops 262144 | bytes 1048576 | tf_op jit(solution)/shard_map/stack | solution.py:161
  1.9 3.5 %collective-permute-start = (bf16[2,512,2,128]{3,2,1,0:T(2,128)(2,1)S(1)}, bf16[2,512,2,128]{3,2,1,0:T(2,128)(2,1)S(1)}, u32[]{:S(2)}, u32[]{:S(2)}) collective-permute-start(bf16[2,512,2,128]{3,2,1,0:T(2,128)(2,1)S(1)} %pad_maximum_fusion), channel_id=1, source_target_pairs={{0,4},{4,8},{8,12},{1,5},{5,9},{9,13},{2,6},{6,10},{10,14},{3,7},{... | collective-permute-start | bytes 1572872 | tf_op jit(solution)/shard_map/ppermute | solution.py:14
  5.4 0.8 %reduce-window.9 = s32[4,1]{0,1:T(1,128)S(1)} reduce-window(s32[4,1]{0,1:T(1,128)} %bitcast.13, s32[]{:T(128)} %constant.4.clone.1), window={size=4x1 pad=3_0x0_0}, to_apply=%region_0.0 | reduce-window | flops 12 | bytes 36 | tf_op jit(solution)/shard_map/reduce-window.4
  6.2 0.7 %bitcast_subtract_fusion = (s32[4]{0:T(128)S(1)}, s32[4]{0:T(128)S(1)}) fusion(s32[4]{0:T(128)} %param.7, s32[4,1]{0,1:T(1,128)S(1)} %reduce-window.9, s32[]{:T(128)S(6)} %mul.3), kind=kLoop, calls=%fused_computation.3 | loop fusion | flops 8 | bytes 68 | tf_op jit(solution)/shard_map/sub | solution.py:137
  6.9 10.6 %collective-permute-done = bf16[2,512,2,128]{3,2,1,0:T(2,128)(2,1)S(1)} collective-permute-done((bf16[2,512,2,128]{3,2,1,0:T(2,128)(2,1)S(1)}, bf16[2,512,2,128]{3,2,1,0:T(2,128)(2,1)S(1)}, u32[]{:S(2)}, u32[]{:S(2)}) %collective-permute-start) | collective-permute-done | bytes 524320 | tf_op jit(solution)/shard_map/ppermute | solution.py:14
  17.5 0.3 slice.4
  17.8 3.5 %collective-permute-start.1 = (bf16[2,384,2,128]{3,2,1,0:T(2,128)(2,1)S(1)}, bf16[2,384,2,128]{3,2,1,0:T(2,128)(2,1)S(1)}, u32[]{:S(2)}, u32[]{:S(2)}) collective-permute-start(bf16[2,384,2,128]{3,2,1,0:T(2,128)(2,1)S(1)} %slice.4), channel_id=1, source_target_pairs={{0,4},{4,8},{8,12},{1,5},{5,9},{9,13},{2,6},{6,10},{10,14},{3,7},{... | collective-permute-start | bytes 1179656 | tf_op jit(solution)/shard_map/ppermute | solution.py:14
  21.2 0.2 select_reduce_fusion
  21.4 1.1 %stack_reshape.6 = bf16[1,512,256]{2,1,0:T(8,128)(2,1)S(1)} reshape(bf16[512,2,128]{2,1,0:T(2,128)(2,1)} %param.5) | data formatting | bytes 524288 | tf_op jit(solution)/shard_map/stack;reshape | solution.py:162
  22.6 0.0 copy-done.1
  22.6 0.2 stack_reshape.7
  22.7 0.0 copy-done
  22.8 1.2 %copy.5 = bf16[64,8,2,512]{3,1,2,0:T(8,128)(2,1)} copy(bf16[64,8,2,512]{3,2,1,0:T(2,128)(2,1)S(1)} %bitcast.10) | data formatting | bytes 2097152
  24.0 0.8 %pad_maximum_fusion.1.kv_ref = bf16[2,512,256]{2,1,0:T(8,128)(2,1)} fusion(bf16[1,512,256]{2,1,0:T(8,128)(2,1)S(1)} %stack_reshape.7, bf16[1,512,256]{2,1,0:T(8,128)(2,1)S(1)} %stack_reshape.6), kind=kLoop, calls=%fused_computation.1 | loop fusion | flops 262144 | bytes 1048576 | tf_op jit(solution)/shard_map/stack | solution.py:162
  24.8 0.5 %broadcast_subtract_fusion.rel_ref = s32[4]{0:T(128)} fusion(s32[4]{0:T(128)S(1)} %select_reduce_fusion, s32[]{:T(128)S(6)} %mul.3), kind=kLoop, calls=%fused_computation.5 | loop fusion | flops 4 | bytes 36 | tf_op jit(solution)/shard_map/sub | solution.py:155
  25.3 6.3 %shard_map.46 = (f32[2,4,128,512]{3,2,1,0:T(8,128)}, f32[2,4,512]{2,1,0:T(4,128)}, f32[2,4,512]{2,1,0:T(4,128)}) custom-call(s32[4]{0:T(128)} %broadcast_subtract_fusion.rel_ref, bf16[512,1024]{1,0:T(8,128)(2,1)} %bitcast.7, bf16[2,512,256]{2,1,0:T(8,128)(2,1)} %pad_maximum_fusion.1.kv_ref), custom_call_target="tpu_custom_call" | custom-call | tf_op jit(solution)/shard_map/pallas_call | solution.py:200
  31.6 1.1 %reshape.47.kv_ref = bf16[2,512,256]{2,1,0:T(8,128)(2,1)} reshape(bf16[2,512,2,128]{3,2,1,0:T(2,128)(2,1)S(1)} %collective-permute-done) | data formatting | bytes 1048576 | tf_op jit(solution)/shard_map/reshape | solution.py:168
  32.8 8.5 %shard_map.47 = (f32[2,4,128,512]{3,2,1,0:T(8,128)}, f32[2,4,512]{2,1,0:T(4,128)}, f32[2,4,512]{2,1,0:T(4,128)}) custom-call(s32[4]{0:T(128)} %broadcast_subtract_fusion.rel_ref, bf16[512,1024]{1,0:T(8,128)(2,1)} %bitcast.8, bf16[2,512,256]{2,1,0:T(8,128)(2,1)} %reshape.47.kv_ref, f32[2,4,128,512]{3,2,1,0:T(8,128)} %get-tuple-element.11.refs_0_, ...), custom_call_target="tpu_custom_call" | custom-call | tf_op jit(solution)/shard_map/pallas_call | solution.py:200
  41.2 0.0 collective-permute-done.1
  41.3 1.0 %reshape.46.kv_ref = bf16[2,384,256]{2,1,0:T(8,128)(2,1)} reshape(bf16[2,384,2,128]{3,2,1,0:T(2,128)(2,1)S(1)} %collective-permute-done.1) | data formatting | bytes 786432 | tf_op jit(solution)/shard_map/reshape | solution.py:168
  42.3 4.1 %shard_map.48 = bf16[512,1024]{1,0:T(8,128)(2,1)} custom-call(s32[4]{0:T(128)} %broadcast_subtract_fusion.rel_ref, bf16[512,1024]{1,0:T(8,128)(2,1)} %bitcast.9, bf16[2,384,256]{2,1,0:T(8,128)(2,1)} %reshape.46.kv_ref, f32[2,4,128,512]{3,2,1,0:T(8,128)} %get-tuple-element.14.refs_0_, f32[2,4,512]{2,1,0:T(4,128)} %get-tuple-element.15.refs_1_, ...), custom_call_target="tpu_custom_call" | custom-call | tf_op jit(solution)/shard_map/pallas_call | solution.py:200
  46.3 2.6 %reshape.48 = bf16[512,2,512]{2,1,0:T(2,128)(2,1)} reshape(bf16[512,1024]{1,0:T(8,128)(2,1)} %shard_map.48) | data formatting | bytes 2097152 | tf_op jit(solution)/shard_map/reshape | solution.py:216
Async XLA Ops:
  0.0 22.6 %copy-start.1 = (bf16[512,2,128]{2,1,0:T(2,128)(2,1)S(1)}, bf16[512,2,128]{2,1,0:T(2,128)(2,1)}, u32[]{:S(2)}) copy-start(bf16[512,2,128]{2,1,0:T(2,128)(2,1)} %param.6) | copy-start | bytes 786436
  0.0 22.7 %copy-start = (bf16[512,2,512]{2,1,0:T(2,128)(2,1)S(1)}, bf16[512,2,512]{2,1,0:T(2,128)(2,1)}, u32[]{:S(2)}) copy-start(bf16[512,2,512]{2,1,0:T(2,128)(2,1)} %param.4) | copy-start | bytes 3145732
  1.9 15.6 %collective-permute-start = (bf16[2,512,2,128]{3,2,1,0:T(2,128)(2,1)S(1)}, bf16[2,512,2,128]{3,2,1,0:T(2,128)(2,1)S(1)}, u32[]{:S(2)}, u32[]{:S(2)}) collective-permute-start(bf16[2,512,2,128]{3,2,1,0:T(2,128)(2,1)S(1)} %pad_maximum_fusion), channel_id=1, source_target_pairs={{0,4},{4,8},{8,12},{1,5},{5,9},{9,13},{2,6},{6,10},{10,14},{3,7},{... | collective-permute-start | bytes 1572872 | tf_op jit(solution)/shard_map/ppermute | solution.py:14
  17.8 23.5 %collective-permute-start.1 = (bf16[2,384,2,128]{3,2,1,0:T(2,128)(2,1)S(1)}, bf16[2,384,2,128]{3,2,1,0:T(2,128)(2,1)S(1)}, u32[]{:S(2)}, u32[]{:S(2)}) collective-permute-start(bf16[2,384,2,128]{3,2,1,0:T(2,128)(2,1)S(1)} %slice.4), channel_id=1, source_target_pairs={{0,4},{4,8},{8,12},{1,5},{5,9},{9,13},{2,6},{6,10},{10,14},{3,7},{... | collective-permute-start | bytes 1179656 | tf_op jit(solution)/shard_map/ppermute | solution.py:14

commit v4 on v2

--- a/solution.py
+++ b/solution.py
@@ -34,27 +34,46 @@
     return regions
 
 
-def make_stage(stage, first, last, dev_blocks, doc_blk, firsts, groups, head_dim, score_scale):
+def make_stage(stage, first, last, heads, dev_blocks, doc_blk, firsts, groups, head_dim, score_scale):
     def local_index(rel):
         if stage == 0:
             return rel
         return rel + stage * dev_blocks - firsts[stage]
 
-    def kernel(rel_ref, q_ref, kv_ref, *refs):
-        k_ref = kv_ref.at[0]
-        v_ref = kv_ref.at[1]
+    def kernel(rel_ref, q_all, kv_all, *refs):
         if first:
             acc_in = m_in = l_in = None
             rest = refs
         else:
             acc_in, m_in, l_in = refs[:3]
             rest = refs[3:]
+        o_sc = None
         if last:
             o_ref = rest[0]
-            (s_sc,) = rest[1:]
+            s_sc, o_sc = rest[1:]
         else:
             acc_out, m_out, l_out = rest[:3]
             (s_sc,) = rest[3:]
+        for hh in range(heads):
+            head_body(hh, rel_ref, q_all, kv_all, acc_in, m_in, l_in,
+                      None if last else acc_out, None if last else m_out, None if last else l_out,
+                      s_sc, o_sc)
+        if last:
+            for i in range(dev_blocks):
+                for g in range(groups):
+                    vals = jnp.stack([o_sc[hh, i, g * BLK : (g + 1) * BLK, :] for hh in range(heads)], axis=1)
+                    o_ref[i * BLK : (i + 1) * BLK, :, g * head_dim : (g + 1) * head_dim] = vals.astype(o_ref.dtype)
+
+    def head_body(hh, rel_ref, q_all, kv_all, acc_in_all, m_in_all, l_in_all, acc_out_all, m_out_all, l_out_all, s_sc, o_sc):
+        q_ref = q_all.at[:, hh * groups * head_dim : (hh + 1) * groups * head_dim]
+        k_ref = kv_all.at[0, :, hh * head_dim : (hh + 1) * head_dim]
+        v_ref = kv_all.at[1, :, hh * head_dim : (hh + 1) * head_dim]
+        acc_in = None if first else acc_in_all.at[hh]
+        m_in = None if first else m_in_all.at[hh]
+        l_in = None if first else l_in_all.at[hh]
+        acc_out = None if last else acc_out_all.at[hh]
+        m_out = None if last else m_out_all.at[hh]
+        l_out = None if last else l_out_all.at[hh]
 
         for i in range(dev_blocks):
             start = rel_ref[i]
@@ -62,11 +81,7 @@
 
             def finish(m_new, row_sum, acc):
                 if last:
-                    out = jnp.transpose(acc * (1.0 / row_sum))
-                    for g in range(groups):
-                        o_ref[i * BLK : (i + 1) * BLK, g * head_dim : (g + 1) * head_dim] = out[
-                            g * BLK : (g + 1) * BLK
-                        ].astype(o_ref.dtype)
+                    o_sc[hh, i] = jnp.transpose(acc * (1.0 / row_sum))
                 else:
                     acc_out[i] = acc
                     m_out[i : i + 1, :] = m_new
@@ -173,27 +188,27 @@
         jax.ShapeDtypeStruct((heads, dev_blocks, rows), jnp.float32),
     )
     state_specs = [
-        pl.BlockSpec((None, dev_blocks, head_dim, rows), lambda h, rel: (h, 0, 0, 0)),
-        pl.BlockSpec((None, dev_blocks, rows), lambda h, rel: (h, 0, 0)),
-        pl.BlockSpec((None, dev_blocks, rows), lambda h, rel: (h, 0, 0)),
+        pl.BlockSpec((heads, dev_blocks, head_dim, rows), lambda h, rel: (0, 0, 0, 0)),
+        pl.BlockSpec((heads, dev_blocks, rows), lambda h, rel: (0, 0, 0)),
+        pl.BlockSpec((heads, dev_blocks, rows), lambda h, rel: (0, 0, 0)),
     ]
     scratch = [
         pltpu.VMEM((max(1, (dev_blocks + 1) // 2), 2 * BLK, rows), jnp.float32),
     ]
-    q_spec = pl.BlockSpec((tok_rows, qwidth), lambda h, rel: (0, h))
+    q_spec = pl.BlockSpec((tok_rows, heads * qwidth), lambda h, rel: (0, 0))
 
     state = None
     out = None
     for stage in range(reach + 1):
         first = stage == 0
         last = stage == reach
-        kernel = make_stage(stage, first, last, dev_blocks, doc_blk, firsts, groups, head_dim, score_scale)
-        kv_spec = pl.BlockSpec((2, kv_src[stage].shape[1], head_dim), lambda h, rel: (0, 0, h))
+        kernel = make_stage(stage, first, last, heads, dev_blocks, doc_blk, firsts, groups, head_dim, score_scale)
+        kv_spec = pl.BlockSpec((2, kv_src[stage].shape[1], heads * head_dim), lambda h, rel: (0, 0, 0))
         in_specs = [q_spec, kv_spec] + ([] if first else state_specs)
         args = [rel_start, q2, kv_src[stage]] + ([] if first else list(state))
         if last:
-            out_shape = jax.ShapeDtypeStruct((tok_rows, heads * qwidth), queries.dtype)
-            out_specs = q_spec
+            out_shape = jax.ShapeDtypeStruct((tok_rows, heads, qwidth), queries.dtype)
+            out_specs = pl.BlockSpec((tok_rows, heads, qwidth), lambda h, rel: (0, 0, 0))
         else:
             out_shape = state_shapes
             out_specs = state_specs
@@ -202,10 +217,10 @@
             out_shape=out_shape,
             grid_spec=pltpu.PrefetchScalarGridSpec(
                 num_scalar_prefetch=1,
-                grid=(heads,),
+                grid=(1,),
                 in_specs=in_specs,
                 out_specs=out_specs,
-                scratch_shapes=scratch,
+                scratch_shapes=scratch + ([pltpu.VMEM((heads, dev_blocks, rows, head_dim), jnp.float32)] if last else []),
             ),
             compiler_params=pltpu.CompilerParams(dimension_semantics=("arbitrary",)),
         )(*args)
@@ -213,7 +228,7 @@
             out = res
         else:
             state = res
-    return out.reshape(tok_rows, heads, qwidth)
+    return out
 
 
 def solution(mesh):

time: 46 us -> 47.5 us (1.033)
  the two profiles are of different devices: /device:TPU:14 before, /device:TPU:8 now
where the time goes in v4:
time: 47.5 us; the launch traced here: 47.2 us
  Pallas kernels  23 us (48%)
  waiting for transfers between devices  11.9 us (25%)
  starting transfers between devices  6.97 us (15%)
  local copies, waits for them, and re-layouts  4.38 us (9%)
  other arithmetic  0.97 us (2%)
    pallas_call x3, Pallas kernels, on_device(): pl.pallas_call(kernel, out_shape=out_shape, grid_spec=pltpu.PrefetchScala...  23 us
    ppermute x2, waiting for transfers between devices, shift_up(): return lax.ppermute(block, axis, [(i, i + 1) for i in range(size - 1)])  11.9 us
    ppermute x2, starting transfers between devices, shift_up(): return lax.ppermute(block, axis, [(i, i + 1) for i in range(size - 1)])  6.97 us
    another operation x3, local copies, waits for them, and re-layouts, on_device(): kv_cur = jnp.stack([k2, v2])  2.35 us
    unnamed x12, local copies, waits for them, and re-layouts  2 us
  transfers between devices with their start and end apart: 2, of which 1 were waited for; matrix products, arithmetic and copies ran while one was open for 5% of the time, Pallas kernels for 34%

profile of v4, /device:TPU:8, one launch (start us, length us, event | category | flops | bytes accessed | tf_op | source)
XLA Modules:
  0.0 47.2 jit_solution(1502806186203650803)
XLA Ops:
  0.0 0.0 copy-start.4
  0.0 0.0 copy-start.2
  0.0 1.2 %stack_reshape.6 = bf16[1,512,256]{2,1,0:T(8,128)(2,1)S(1)} reshape(bf16[512,2,128]{2,1,0:T(2,128)(2,1)} %param.5) | data formatting | bytes 524288 | tf_op jit(solution)/shard_map/stack;reshape | solution.py:176
  1.2 1.1 %stack_reshape.7 = bf16[1,512,256]{2,1,0:T(8,128)(2,1)S(1)} reshape(bf16[512,2,128]{2,1,0:T(2,128)(2,1)} %param.6) | data formatting | bytes 524288 | tf_op jit(solution)/shard_map/stack;reshape | solution.py:176
  2.4 0.0 copy-start.1
  2.4 3.5 %collective-permute-start = (bf16[2,512,256]{2,1,0:T(8,128)(2,1)S(1)}, bf16[2,512,256]{2,1,0:T(8,128)(2,1)S(1)}, u32[]{:S(2)}, u32[]{:S(2)}) collective-permute-start(bf16[2,512,256]{2,1,0:T(8,128)(2,1)S(1)} %constant_dynamic-update-slice_fusion.kv_all), channel_id=1, source_target_pairs={{0,4},{4,8},{8,12},{1,5},{5,9},{9,13},{2,6},{6,10},{10,14},{3,7},{... | collective-permute-start | bytes 1572872 | tf_op jit(solution)/shard_map/ppermute | solution.py:14
  5.9 0.0 copy-done.4
  5.9 0.2 reduce-window.9
  6.1 11.9 %collective-permute-done.kv_all = bf16[2,512,256]{2,1,0:T(8,128)(2,1)S(1)} collective-permute-done((bf16[2,512,256]{2,1,0:T(8,128)(2,1)S(1)}, bf16[2,512,256]{2,1,0:T(8,128)(2,1)S(1)}, u32[]{:S(2)}, u32[]{:S(2)}) %collective-permute-start) | collective-permute-done | bytes 524320 | tf_op jit(solution)/shard_map/ppermute | solution.py:14
  18.0 0.0 copy-start
  18.0 3.5 %collective-permute-start.1 = (bf16[2,384,256]{2,1,0:T(8,128)(2,1)S(1)}, bf16[2,384,256]{2,1,0:T(8,128)(2,1)S(1)}, u32[]{:S(2)}, u32[]{:S(2)}) collective-permute-start(bf16[2,384,256]{2,1,0:T(8,128)(2,1)S(1)} %slice.4), channel_id=1, source_target_pairs={{0,4},{4,8},{8,12},{1,5},{5,9},{9,13},{2,6},{6,10},{10,14},{3,7},{... | collective-permute-start | bytes 1179656 | tf_op jit(solution)/shard_map/ppermute | solution.py:14
  21.5 0.0 copy-done.2
  21.5 1.2 %copy.5 = bf16[64,8,2,512]{3,1,2,0:T(8,128)(2,1)} copy(bf16[64,8,2,512]{3,2,1,0:T(2,128)(2,1)S(1)} %bitcast.8) | data formatting | bytes 2097152
  22.7 0.2 select_reduce_fusion
  22.9 0.6 %broadcast_subtract_fusion.rel_ref = s32[4]{0:T(128)} fusion(s32[4]{0:T(128)S(1)} %select_reduce_fusion, s32[]{:T(128)S(6)} %mul.3), kind=kLoop, calls=%fused_computation.5 | loop fusion | flops 4 | bytes 36 | tf_op jit(solution)/shard_map/sub | solution.py:170
  23.5 0.0 copy-done.1
  23.5 6.7 %shard_map.46 = (f32[2,4,128,512]{3,2,1,0:T(8,128)}, f32[2,4,512]{2,1,0:T(4,128)}, f32[2,4,512]{2,1,0:T(4,128)}) custom-call(s32[4]{0:T(128)} %broadcast_subtract_fusion.rel_ref, bf16[512,1024]{1,0:T(8,128)(2,1)} %bitcast.5, bf16[2,512,256]{2,1,0:T(8,128)(2,1)} %copy-done.1), custom_call_target="tpu_custom_call" | custom-call | tf_op jit(solution)/shard_map/pallas_call | solution.py:215
  30.2 0.0 copy-done
  30.2 9.3 %shard_map.47 = (f32[2,4,128,512]{3,2,1,0:T(8,128)}, f32[2,4,512]{2,1,0:T(4,128)}, f32[2,4,512]{2,1,0:T(4,128)}) custom-call(s32[4]{0:T(128)} %broadcast_subtract_fusion.rel_ref, bf16[512,1024]{1,0:T(8,128)(2,1)} %bitcast.6, bf16[2,512,256]{2,1,0:T(8,128)(2,1)} %copy-done, f32[2,4,128,512]{3,2,1,0:T(8,128)} %get-tuple-element.11.refs_0_, ...), custom_call_target="tpu_custom_call" | custom-call | tf_op jit(solution)/shard_map/pallas_call | solution.py:215
  39.6 0.0 collective-permute-done.1.kv_all
  39.6 0.0 copy-start.3
  39.6 0.7 %copy-done.3 = bf16[2,384,256]{2,1,0:T(8,128)(2,1)} copy-done((bf16[2,384,256]{2,1,0:T(8,128)(2,1)}, bf16[2,384,256]{2,1,0:T(8,128)(2,1)S(1)}, u32[]{:S(2)}) %copy-start.3) | copy-done | bytes 393240
  40.3 6.9 %shard_map.48 = bf16[512,2,512]{2,1,0:T(2,128)(2,1)} custom-call(s32[4]{0:T(128)} %broadcast_subtract_fusion.rel_ref, bf16[512,1024]{1,0:T(8,128)(2,1)} %bitcast.7, bf16[2,384,256]{2,1,0:T(8,128)(2,1)} %copy-done.3, f32[2,4,128,512]{3,2,1,0:T(8,128)} %get-tuple-element.14.refs_0_, f32[2,4,512]{2,1,0:T(4,128)} %get-tuple-element.15.refs_1_, ...), custom_call_target="tpu_custom_call" | custom-call | tf_op jit(solution)/shard_map/pallas_call | solution.py:215
  (4 shorter events, 0.1 us)
Async XLA Ops:
  0.0 5.9 %copy-start.4 = (s32[4]{0:T(128)S(1)}, s32[4]{0:T(128)}, u32[]{:S(2)}) copy-start(s32[4]{0:T(128)} %param.7) | copy-start | bytes 52
  0.0 21.5 %copy-start.2 = (bf16[512,2,512]{2,1,0:T(2,128)(2,1)S(1)}, bf16[512,2,512]{2,1,0:T(2,128)(2,1)}, u32[]{:S(2)}) copy-start(bf16[512,2,512]{2,1,0:T(2,128)(2,1)} %param.4) | copy-start | bytes 3145732
  2.4 21.1 %copy-start.1 = (bf16[2,512,256]{2,1,0:T(8,128)(2,1)}, bf16[2,512,256]{2,1,0:T(8,128)(2,1)S(1)}, u32[]{:S(2)}) copy-start(bf16[2,512,256]{2,1,0:T(8,128)(2,1)S(1)} %constant_dynamic-update-slice_fusion.kv_all) | copy-start | bytes 1572868
  2.4 15.6 %collective-permute-start = (bf16[2,512,256]{2,1,0:T(8,128)(2,1)S(1)}, bf16[2,512,256]{2,1,0:T(8,128)(2,1)S(1)}, u32[]{:S(2)}, u32[]{:S(2)}) collective-permute-start(bf16[2,512,256]{2,1,0:T(8,128)(2,1)S(1)} %constant_dynamic-update-slice_fusion.kv_all), channel_id=1, source_target_pairs={{0,4},{4,8},{8,12},{1,5},{5,9},{9,13},{2,6},{6,10},{10,14},{3,7},{... | collective-permute-start | bytes 1572872 | tf_op jit(solution)/shard_map/ppermute | solution.py:14
  18.0 12.3 %copy-start = (bf16[2,512,256]{2,1,0:T(8,128)(2,1)}, bf16[2,512,256]{2,1,0:T(8,128)(2,1)S(1)}, u32[]{:S(2)}) copy-start(bf16[2,512,256]{2,1,0:T(8,128)(2,1)S(1)} %collective-permute-done.kv_all) | copy-start | bytes 1572868
  18.0 21.6 %collective-permute-start.1 = (bf16[2,384,256]{2,1,0:T(8,128)(2,1)S(1)}, bf16[2,384,256]{2,1,0:T(8,128)(2,1)S(1)}, u32[]{:S(2)}, u32[]{:S(2)}) collective-permute-start(bf16[2,384,256]{2,1,0:T(8,128)(2,1)S(1)} %slice.4), channel_id=1, source_target_pairs={{0,4},{4,8},{8,12},{1,5},{5,9},{9,13},{2,6},{6,10},{10,14},{3,7},{... | collective-permute-start | bytes 1179656 | tf_op jit(solution)/shard_map/ppermute | solution.py:14
  39.6 0.7 %copy-start.3 = (bf16[2,384,256]{2,1,0:T(8,128)(2,1)}, bf16[2,384,256]{2,1,0:T(8,128)(2,1)S(1)}, u32[]{:S(2)}) copy-start(bf16[2,384,256]{2,1,0:T(8,128)(2,1)S(1)} %collective-permute-done.1.kv_all) | copy-start | bytes 1179652

commit v5 on v2

--- a/solution.py
+++ b/solution.py
@@ -161,8 +161,16 @@
     kv_cur = jnp.stack([k2, v2])
     kv_src = [kv_cur]
     prev_first = 0
+    split = firsts[2] * BLK if reach >= 2 else 0
     for r in range(1, reach + 1):
         cut = (firsts[r] - prev_first) * BLK
+        if r == 1 and split > 0:
+            tail = shift_up(kv_cur[:, split:], "seq")
+            head = shift_up(kv_cur[:, :split], "seq")
+            kv_src.append(jnp.concatenate([head, tail], axis=1))
+            kv_cur = tail
+            prev_first = firsts[2]
+            continue
         kv_cur = shift_up(kv_cur[:, cut:], "seq")
         prev_first = firsts[r]
         kv_src.append(kv_cur)

time: 46 us -> 45.2 us (0.983)
  the two profiles are of different devices: /device:TPU:14 before, /device:TPU:12 now
where the time goes in v5:
time: 45.2 us; the launch traced here: 44.9 us
  Pallas kernels  18.9 us (42%)
  starting transfers between devices  10.4 us (23%)
  local copies, waits for them, and re-layouts  6.99 us (15%)
  waiting for transfers between devices  6.68 us (15%)
  other arithmetic  1.82 us (4%)
    pallas_call x3, Pallas kernels, on_device(): pl.pallas_call(kernel, out_shape=out_shape, grid_spec=pltpu.PrefetchScala...  18.9 us
    ppermute x3, starting transfers between devices, shift_up(): return lax.ppermute(block, axis, [(i, i + 1) for i in range(size - 1)])  10.4 us
    ppermute x3, waiting for transfers between devices, shift_up(): return lax.ppermute(block, axis, [(i, i + 1) for i in range(size - 1)])  6.68 us
    reshape x1, local copies, waits for them, and re-layouts, on_device(): return out.reshape(tok_rows, heads, qwidth)  2.62 us
    another operation x3, local copies, waits for them, and re-layouts, on_device(): kv_cur = jnp.stack([k2, v2])  2.35 us
    unnamed x10, local copies, waits for them, and re-layouts  1.99 us
  transfers between devices with their start and end apart: 3, of which 1 were waited for; matrix products, arithmetic and copies ran while one was open for 7% of the time, Pallas kernels for 33%

profile of v5, /device:TPU:12, one launch (start us, length us, event | category | flops | bytes accessed | tf_op | source)
XLA Modules:
  0.0 44.9 jit_solution(4069442007758317952)
XLA Ops:
  0.0 0.0 copy-start.3
  0.0 1.2 %stack_reshape.6 = bf16[1,512,256]{2,1,0:T(8,128)(2,1)S(1)} reshape(bf16[512,2,128]{2,1,0:T(2,128)(2,1)} %param.5) | data formatting | bytes 524288 | tf_op jit(solution)/shard_map/stack;reshape | solution.py:161
  1.2 1.1 %stack_reshape.7 = bf16[1,512,256]{2,1,0:T(8,128)(2,1)S(1)} reshape(bf16[512,2,128]{2,1,0:T(2,128)(2,1)} %param.6) | data formatting | bytes 524288 | tf_op jit(solution)/shard_map/stack;reshape | solution.py:161
  2.4 0.0 copy-start
  2.4 3.5 %collective-permute-start = (bf16[2,384,256]{2,1,0:T(8,128)(2,1)S(1)}, bf16[2,384,256]{2,1,0:T(8,128)(2,1)S(1)}, u32[]{:S(2)}, u32[]{:S(2)}) collective-permute-start(bf16[2,384,256]{2,1,0:T(8,128)(2,1)S(1)} %slice.8), channel_id=1, source_target_pairs={{0,4},{4,8},{8,12},{1,5},{5,9},{9,13},{2,6},{6,10},{10,14},{3,7},{... | collective-permute-start | bytes 1179656 | tf_op jit(solution)/shard_map/ppermute | solution.py:14
  5.9 3.5 %collective-permute-start.2 = (bf16[2,128,256]{2,1,0:T(8,128)(2,1)S(1)}, bf16[2,128,256]{2,1,0:T(8,128)(2,1)S(1)}, u32[]{:S(2)}, u32[]{:S(2)}) collective-permute-start(bf16[2,128,256]{2,1,0:T(8,128)(2,1)S(1)} %slice.9), channel_id=1, source_target_pairs={{0,4},{4,8},{8,12},{1,5},{5,9},{9,13},{2,6},{6,10},{10,14},{3,7},{... | collective-permute-start | bytes 393224 | tf_op jit(solution)/shard_map/ppermute | solution.py:14
  9.4 0.0 copy-done.3
  9.5 0.2 reduce-window.9
  9.6 6.7 %collective-permute-done = bf16[2,384,256]{2,1,0:T(8,128)(2,1)S(1)} collective-permute-done((bf16[2,384,256]{2,1,0:T(8,128)(2,1)S(1)}, bf16[2,384,256]{2,1,0:T(8,128)(2,1)S(1)}, u32[]{:S(2)}, u32[]{:S(2)}) %collective-permute-start) | collective-permute-done | bytes 393248 | tf_op jit(solution)/shard_map/ppermute | solution.py:14
  16.3 3.5 %collective-permute-start.1 = (bf16[2,384,256]{2,1,0:T(8,128)(2,1)S(1)}, bf16[2,384,256]{2,1,0:T(8,128)(2,1)S(1)}, u32[]{:S(2)}, u32[]{:S(2)}) collective-permute-start(bf16[2,384,256]{2,1,0:T(8,128)(2,1)S(1)} %collective-permute-done), channel_id=1, source_target_pairs={{0,4},{4,8},{8,12},{1,5},{5,9},{9,13},{2,6},{6,10},{10,14},{3,7},{... | collective-permute-start | bytes 1179656 | tf_op jit(solution)/shard_map/ppermute | solution.py:14
  19.8 0.2 select_reduce_fusion
  20.0 0.0 copy-done.1
  20.0 1.2 %copy.5 = bf16[64,8,2,512]{3,1,2,0:T(8,128)(2,1)} copy(bf16[64,8,2,512]{3,2,1,0:T(2,128)(2,1)S(1)} %bitcast.8) | data formatting | bytes 2097152
  21.2 0.6 %broadcast_subtract_fusion.rel_ref = s32[4]{0:T(128)} fusion(s32[4]{0:T(128)S(1)} %select_reduce_fusion, s32[]{:T(128)S(6)} %mul.3), kind=kLoop, calls=%fused_computation.6 | loop fusion | flops 4 | bytes 36 | tf_op jit(solution)/shard_map/sub | solution.py:155
  21.8 0.0 copy-done
  21.8 6.3 %shard_map.46 = (f32[2,4,128,512]{3,2,1,0:T(8,128)}, f32[2,4,512]{2,1,0:T(4,128)}, f32[2,4,512]{2,1,0:T(4,128)}) custom-call(s32[4]{0:T(128)} %broadcast_subtract_fusion.rel_ref, bf16[512,1024]{1,0:T(8,128)(2,1)} %bitcast.5, bf16[2,512,256]{2,1,0:T(8,128)(2,1)} %copy-done), custom_call_target="tpu_custom_call" | custom-call | tf_op jit(solution)/shard_map/pallas_call | solution.py:208
  28.1 0.0 collective-permute-done.2
  28.1 0.9 %pad_maximum_fusion.kv_ref = bf16[2,512,256]{2,1,0:T(8,128)(2,1)} fusion(bf16[2,384,256]{2,1,0:T(8,128)(2,1)S(1)} %collective-permute-done, bf16[2,128,256]{2,1,0:T(8,128)(2,1)S(1)} %collective-permute-done.2), kind=kLoop, calls=%fused_computation | loop fusion | flops 1048576 | bytes 1048576 | tf_op jit(solution)/shard_map/concatenate | solution.py:170
  29.0 8.5 %shard_map.47 = (f32[2,4,128,512]{3,2,1,0:T(8,128)}, f32[2,4,512]{2,1,0:T(4,128)}, f32[2,4,512]{2,1,0:T(4,128)}) custom-call(s32[4]{0:T(128)} %broadcast_subtract_fusion.rel_ref, bf16[512,1024]{1,0:T(8,128)(2,1)} %bitcast.6, bf16[2,512,256]{2,1,0:T(8,128)(2,1)} %pad_maximum_fusion.kv_ref, f32[2,4,128,512]{3,2,1,0:T(8,128)} %get-tuple-element.11.refs_0_, ...), custom_call_target="tpu_custom_call" | custom-call | tf_op jit(solution)/shard_map/pallas_call | solution.py:208
  37.5 0.0 collective-permute-done.1.kv_ref
  37.5 0.0 copy-start.2
  37.5 0.7 %copy-done.2 = bf16[2,384,256]{2,1,0:T(8,128)(2,1)} copy-done((bf16[2,384,256]{2,1,0:T(8,128)(2,1)}, bf16[2,384,256]{2,1,0:T(8,128)(2,1)S(1)}, u32[]{:S(2)}) %copy-start.2) | copy-done | bytes 393240
  38.2 4.1 %shard_map.48 = bf16[512,1024]{1,0:T(8,128)(2,1)} custom-call(s32[4]{0:T(128)} %broadcast_subtract_fusion.rel_ref, bf16[512,1024]{1,0:T(8,128)(2,1)} %bitcast.7, bf16[2,384,256]{2,1,0:T(8,128)(2,1)} %copy-done.2, f32[2,4,128,512]{3,2,1,0:T(8,128)} %get-tuple-element.14.refs_0_, f32[2,4,512]{2,1,0:T(4,128)} %get-tuple-element.15.refs_1_, ...), custom_call_target="tpu_custom_call" | custom-call | tf_op jit(solution)/shard_map/pallas_call | solution.py:208
  42.3 2.6 %reshape.40 = bf16[512,2,512]{2,1,0:T(2,128)(2,1)} reshape(bf16[512,1024]{1,0:T(8,128)(2,1)} %shard_map.48) | data formatting | bytes 2097152 | tf_op jit(solution)/shard_map/reshape | solution.py:224
  (6 shorter events, 0.1 us)
Async XLA Ops:
  0.0 9.4 %copy-start.3 = (s32[4]{0:T(128)S(1)}, s32[4]{0:T(128)}, u32[]{:S(2)}) copy-start(s32[4]{0:T(128)} %param.7) | copy-start | bytes 52
  0.0 20.0 %copy-start.1 = (bf16[512,2,512]{2,1,0:T(2,128)(2,1)S(1)}, bf16[512,2,512]{2,1,0:T(2,128)(2,1)}, u32[]{:S(2)}) copy-start(bf16[512,2,512]{2,1,0:T(2,128)(2,1)} %param.4) | copy-start | bytes 3145732
  2.4 19.4 %copy-start = (bf16[2,512,256]{2,1,0:T(8,128)(2,1)}, bf16[2,512,256]{2,1,0:T(8,128)(2,1)S(1)}, u32[]{:S(2)}) copy-start(bf16[2,512,256]{2,1,0:T(8,128)(2,1)S(1)} %constant_dynamic-update-slice_fusion.kv_ref) | copy-start | bytes 1572868
  2.4 13.9 %collective-permute-start = (bf16[2,384,256]{2,1,0:T(8,128)(2,1)S(1)}, bf16[2,384,256]{2,1,0:T(8,128)(2,1)S(1)}, u32[]{:S(2)}, u32[]{:S(2)}) collective-permute-start(bf16[2,384,256]{2,1,0:T(8,128)(2,1)S(1)} %slice.8), channel_id=1, source_target_pairs={{0,4},{4,8},{8,12},{1,5},{5,9},{9,13},{2,6},{6,10},{10,14},{3,7},{... | collective-permute-start | bytes 1179656 | tf_op jit(solution)/shard_map/ppermute | solution.py:14
  5.9 22.2 %collective-permute-start.2 = (bf16[2,128,256]{2,1,0:T(8,128)(2,1)S(1)}, bf16[2,128,256]{2,1,0:T(8,128)(2,1)S(1)}, u32[]{:S(2)}, u32[]{:S(2)}) collective-permute-start(bf16[2,128,256]{2,1,0:T(8,128)(2,1)S(1)} %slice.9), channel_id=1, source_target_pairs={{0,4},{4,8},{8,12},{1,5},{5,9},{9,13},{2,6},{6,10},{10,14},{3,7},{... | collective-permute-start | bytes 393224 | tf_op jit(solution)/shard_map/ppermute | solution.py:14
  16.3 21.1 %collective-permute-start.1 = (bf16[2,384,256]{2,1,0:T(8,128)(2,1)S(1)}, bf16[2,384,256]{2,1,0:T(8,128)(2,1)S(1)}, u32[]{:S(2)}, u32[]{:S(2)}) collective-permute-start(bf16[2,384,256]{2,1,0:T(8,128)(2,1)S(1)} %collective-permute-done), channel_id=1, source_target_pairs={{0,4},{4,8},{8,12},{1,5},{5,9},{9,13},{2,6},{6,10},{10,14},{3,7},{... | collective-permute-start | bytes 1179656 | tf_op jit(solution)/shard_map/ppermute | solution.py:14
  37.5 0.7 %copy-start.2 = (bf16[2,384,256]{2,1,0:T(8,128)(2,1)}, bf16[2,384,256]{2,1,0:T(8,128)(2,1)S(1)}, u32[]{:S(2)}) copy-start(bf16[2,384,256]{2,1,0:T(8,128)(2,1)S(1)} %collective-permute-done.1.kv_ref) | copy-start | bytes 1179652

commit v6 on v3

--- a/solution.py
+++ b/solution.py
@@ -9,9 +9,9 @@
 BLK = 128
 
 
-def shift_up(block, axis):
+def shift_up(block, axis, distance=1):
     size = lax.axis_size(axis)
-    return lax.ppermute(block, axis, [(i, i + 1) for i in range(size - 1)])
+    return lax.ppermute(block, axis, [(i, i + distance) for i in range(size - distance)])
 
 
 def first_needed(distance, reach, dev_blocks):
@@ -158,14 +158,10 @@
     k2 = keys.reshape(tok_rows, heads * head_dim)
     v2 = values.reshape(tok_rows, heads * head_dim)
 
-    kv_cur = jnp.stack([keys, values])
-    kv_src = [jnp.stack([k2, v2])]
-    prev_first = 0
+    kv_own = jnp.stack([k2, v2])
+    kv_src = [kv_own]
     for r in range(1, reach + 1):
-        cut = (firsts[r] - prev_first) * BLK
-        kv_cur = shift_up(kv_cur[:, cut:], "seq")
-        prev_first = firsts[r]
-        kv_src.append(kv_cur.reshape(2, kv_cur.shape[1], heads * head_dim))
+        kv_src.append(shift_up(kv_own[:, firsts[r] * BLK :], "seq", r))
 
     state_shapes = (
         jax.ShapeDtypeStruct((heads, dev_blocks, head_dim, rows), jnp.float32),

time: 49.3 us -> 43.9 us (0.89)
  the two profiles are of different devices: /device:TPU:8 before, /device:TPU:16 now
where the time goes in v6:
time: 43.9 us; the launch traced here: 43.7 us
  Pallas kernels  18.2 us (41%)
  waiting for transfers between devices  11.8 us (27%)
  local copies, waits for them, and re-layouts  7.8 us (18%)
  starting transfers between devices  4.78 us (11%)
  other arithmetic  0.96 us (2%)
    pallas_call x3, Pallas kernels, on_device(): pl.pallas_call(kernel, out_shape=out_shape, grid_spec=pltpu.PrefetchScala...  18.2 us
    ppermute x2, waiting for transfers between devices, shift_up(): lax.ppermute(block, axis, [(i, i + distance) for i in range(size - distan...  11.8 us
    ppermute x2, starting transfers between devices, shift_up(): lax.ppermute(block, axis, [(i, i + distance) for i in range(size - distan...  4.78 us
    unnamed x12, local copies, waits for them, and re-layouts  2.81 us
    reshape x1, local copies, waits for them, and re-layouts, on_device(): return out.reshape(tok_rows, heads, qwidth)  2.62 us
    another operation x3, local copies, waits for them, and re-layouts, on_device(): kv_own = jnp.stack([k2, v2])  2.35 us
  transfers between devices with their start and end apart: 2, of which 1 were waited for; matrix products, arithmetic and copies ran while one was open for 5% of the time, Pallas kernels for 28%

profile of v6, /device:TPU:16, one launch (start us, length us, event | category | flops | bytes accessed | tf_op | source)
XLA Modules:
  0.0 43.7 jit_solution(10331207968711222969)
XLA Ops:
  0.0 0.0 copy-start.4
  0.0 0.0 copy-start.1
  0.0 1.2 %stack_reshape.6 = bf16[1,512,256]{2,1,0:T(8,128)(2,1)S(1)} reshape(bf16[512,2,128]{2,1,0:T(2,128)(2,1)} %param.5) | data formatting | bytes 524288 | tf_op jit(solution)/shard_map/stack;reshape | solution.py:161
  1.2 1.1 %stack_reshape.7 = bf16[1,512,256]{2,1,0:T(8,128)(2,1)S(1)} reshape(bf16[512,2,128]{2,1,0:T(2,128)(2,1)} %param.6) | data formatting | bytes 524288 | tf_op jit(solution)/shard_map/stack;reshape | solution.py:161
  2.4 0.0 copy-start
  2.4 3.5 %collective-permute-start.1 = (bf16[2,512,256]{2,1,0:T(8,128)(2,1)S(1)}, bf16[2,512,256]{2,1,0:T(8,128)(2,1)S(1)}, u32[]{:S(2)}, u32[]{:S(2)}) collective-permute-start(bf16[2,512,256]{2,1,0:T(8,128)(2,1)S(1)} %constant_dynamic-update-slice_fusion.kv_ref), channel_id=1, source_target_pairs={{0,4},{4,8},{8,12},{1,5},{5,9},{9,13},{2,6},{6,10},{10,14},{3,7},{... | collective-permute-start | bytes 1572872 | tf_op jit(solution)/shard_map/ppermute | solution.py:14
  5.9 1.3 %collective-permute-start = (bf16[2,384,256]{2,1,0:T(8,128)(2,1)S(1)}, bf16[2,384,256]{2,1,0:T(8,128)(2,1)S(1)}, u32[]{:S(2)}, u32[]{:S(2)}) collective-permute-start(bf16[2,384,256]{2,1,0:T(8,128)(2,1)S(1)} %slice.4), channel_id=1, source_target_pairs={{0,8},{4,12},{1,9},{5,13},{2,10},{6,14},{3,11},{7,15},{16,24},{20,... | collective-permute-start | bytes 1179656 | tf_op jit(solution)/shard_map/ppermute | solution.py:14
  7.2 0.0 copy-done.4
  7.2 0.2 reduce-window.9
  7.4 0.0 copy-done.1
  7.4 1.2 %copy.5 = bf16[64,8,2,512]{3,1,2,0:T(8,128)(2,1)} copy(bf16[64,8,2,512]{3,2,1,0:T(2,128)(2,1)S(1)} %bitcast.8) | data formatting | bytes 2097152
  8.7 0.2 select_reduce_fusion
  8.8 0.6 %broadcast_subtract_fusion.rel_ref = s32[4]{0:T(128)} fusion(s32[4]{0:T(128)S(1)} %select_reduce_fusion, s32[]{:T(128)S(6)} %mul.3), kind=kLoop, calls=%fused_computation.5 | loop fusion | flops 4 | bytes 36 | tf_op jit(solution)/shard_map/sub | solution.py:155
  9.4 0.0 copy-done
  9.4 6.3 %shard_map.46 = (f32[2,4,128,512]{3,2,1,0:T(8,128)}, f32[2,4,512]{2,1,0:T(4,128)}, f32[2,4,512]{2,1,0:T(4,128)}) custom-call(s32[4]{0:T(128)} %broadcast_subtract_fusion.rel_ref, bf16[512,1024]{1,0:T(8,128)(2,1)} %bitcast.5, bf16[2,512,256]{2,1,0:T(8,128)(2,1)} %copy-done), custom_call_target="tpu_custom_call" | custom-call | tf_op jit(solution)/shard_map/pallas_call | solution.py:196
  15.7 11.8 %collective-permute-done.1.kv_ref = bf16[2,512,256]{2,1,0:T(8,128)(2,1)S(1)} collective-permute-done((bf16[2,512,256]{2,1,0:T(8,128)(2,1)S(1)}, bf16[2,512,256]{2,1,0:T(8,128)(2,1)S(1)}, u32[]{:S(2)}, u32[]{:S(2)}) %collective-permute-start.1) | collective-permute-done | bytes 524320 | tf_op jit(solution)/shard_map/ppermute | solution.py:14
  27.5 0.0 copy-start.2
  27.5 0.8 %copy-done.2 = bf16[2,512,256]{2,1,0:T(8,128)(2,1)} copy-done((bf16[2,512,256]{2,1,0:T(8,128)(2,1)}, bf16[2,512,256]{2,1,0:T(8,128)(2,1)S(1)}, u32[]{:S(2)}) %copy-start.2) | copy-done | bytes 524312
  28.3 6.0 %shard_map.47 = (f32[2,4,128,512]{3,2,1,0:T(8,128)}, f32[2,4,512]{2,1,0:T(4,128)}, f32[2,4,512]{2,1,0:T(4,128)}) custom-call(s32[4]{0:T(128)} %broadcast_subtract_fusion.rel_ref, bf16[512,1024]{1,0:T(8,128)(2,1)} %bitcast.6, bf16[2,512,256]{2,1,0:T(8,128)(2,1)} %copy-done.2, f32[2,4,128,512]{3,2,1,0:T(8,128)} %get-tuple-element.11.refs_0_, ...), custom_call_target="tpu_custom_call" | custom-call | tf_op jit(solution)/shard_map/pallas_call | solution.py:196
  34.3 0.0 collective-permute-done.kv_ref
  34.3 0.0 copy-start.3
  34.3 0.7 %copy-done.3 = bf16[2,384,256]{2,1,0:T(8,128)(2,1)} copy-done((bf16[2,384,256]{2,1,0:T(8,128)(2,1)}, bf16[2,384,256]{2,1,0:T(8,128)(2,1)S(1)}, u32[]{:S(2)}) %copy-start.3) | copy-done | bytes 393240
  35.1 6.0 %shard_map.48 = bf16[512,1024]{1,0:T(8,128)(2,1)} custom-call(s32[4]{0:T(128)} %broadcast_subtract_fusion.rel_ref, bf16[512,1024]{1,0:T(8,128)(2,1)} %bitcast.7, bf16[2,384,256]{2,1,0:T(8,128)(2,1)} %copy-done.3, f32[2,4,128,512]{3,2,1,0:T(8,128)} %get-tuple-element.14.refs_0_, f32[2,4,512]{2,1,0:T(4,128)} %get-tuple-element.15.refs_1_, ...), custom_call_target="tpu_custom_call" | custom-call | tf_op jit(solution)/shard_map/pallas_call | solution.py:196
  41.0 2.6 %reshape.40 = bf16[512,2,512]{2,1,0:T(2,128)(2,1)} reshape(bf16[512,1024]{1,0:T(8,128)(2,1)} %shard_map.48) | data formatting | bytes 2097152 | tf_op jit(solution)/shard_map/reshape | solution.py:212
  (4 shorter events, 0.1 us)
Async XLA Ops:
  0.0 7.2 %copy-start.4 = (s32[4]{0:T(128)S(1)}, s32[4]{0:T(128)}, u32[]{:S(2)}) copy-start(s32[4]{0:T(128)} %param.7) | copy-start | bytes 52
  0.0 7.4 %copy-start.1 = (bf16[512,2,512]{2,1,0:T(2,128)(2,1)S(1)}, bf16[512,2,512]{2,1,0:T(2,128)(2,1)}, u32[]{:S(2)}) copy-start(bf16[512,2,512]{2,1,0:T(2,128)(2,1)} %param.4) | copy-start | bytes 3145732
  2.4 7.0 %copy-start = (bf16[2,512,256]{2,1,0:T(8,128)(2,1)}, bf16[2,512,256]{2,1,0:T(8,128)(2,1)S(1)}, u32[]{:S(2)}) copy-start(bf16[2,512,256]{2,1,0:T(8,128)(2,1)S(1)} %constant_dynamic-update-slice_fusion.kv_ref) | copy-start | bytes 1572868
  2.4 25.1 %collective-permute-start.1 = (bf16[2,512,256]{2,1,0:T(8,128)(2,1)S(1)}, bf16[2,512,256]{2,1,0:T(8,128)(2,1)S(1)}, u32[]{:S(2)}, u32[]{:S(2)}) collective-permute-start(bf16[2,512,256]{2,1,0:T(8,128)(2,1)S(1)} %constant_dynamic-update-slice_fusion.kv_ref), channel_id=1, source_target_pairs={{0,4},{4,8},{8,12},{1,5},{5,9},{9,13},{2,6},{6,10},{10,14},{3,7},{... | collective-permute-start | bytes 1572872 | tf_op jit(solution)/shard_map/ppermute | solution.py:14
  5.9 28.4 %collective-permute-start = (bf16[2,384,256]{2,1,0:T(8,128)(2,1)S(1)}, bf16[2,384,256]{2,1,0:T(8,128)(2,1)S(1)}, u32[]{:S(2)}, u32[]{:S(2)}) collective-permute-start(bf16[2,384,256]{2,1,0:T(8,128)(2,1)S(1)} %slice.4), channel_id=1, source_target_pairs={{0,8},{4,12},{1,9},{5,13},{2,10},{6,14},{3,11},{7,15},{16,24},{20,... | collective-permute-start | bytes 1179656 | tf_op jit(solution)/shard_map/ppermute | solution.py:14
  27.5 0.8 %copy-start.2 = (bf16[2,512,256]{2,1,0:T(8,128)(2,1)}, bf16[2,512,256]{2,1,0:T(8,128)(2,1)S(1)}, u32[]{:S(2)}) copy-start(bf16[2,512,256]{2,1,0:T(8,128)(2,1)S(1)} %collective-permute-done.1.kv_ref) | copy-start | bytes 1572868
  34.3 0.7 %copy-start.3 = (bf16[2,384,256]{2,1,0:T(8,128)(2,1)}, bf16[2,384,256]{2,1,0:T(8,128)(2,1)S(1)}, u32[]{:S(2)}) copy-start(bf16[2,384,256]{2,1,0:T(8,128)(2,1)S(1)} %collective-permute-done.kv_ref) | copy-start | bytes 1179652

commit v7 on v2

--- a/solution.py
+++ b/solution.py
@@ -34,7 +34,7 @@
     return regions
 
 
-def make_stage(stage, first, last, dev_blocks, doc_blk, firsts, groups, head_dim, score_scale):
+def make_stage(stage, first, last, provisional, dev_blocks, doc_blk, firsts, groups, head_dim, score_scale):
     def local_index(rel):
         if stage == 0:
             return rel
@@ -52,6 +52,9 @@
         if last:
             o_ref = rest[0]
             (s_sc,) = rest[1:]
+        elif provisional:
+            acc_out, m_out, l_out, o_ref = rest[:4]
+            (s_sc,) = rest[4:]
         else:
             acc_out, m_out, l_out = rest[:3]
             (s_sc,) = rest[3:]
@@ -61,13 +64,13 @@
             regions = stage_regions(stage, i, dev_blocks, doc_blk, firsts)
 
             def finish(m_new, row_sum, acc):
-                if last:
+                if last or provisional:
                     out = jnp.transpose(acc * (1.0 / row_sum))
                     for g in range(groups):
                         o_ref[i * BLK : (i + 1) * BLK, g * head_dim : (g + 1) * head_dim] = out[
                             g * BLK : (g + 1) * BLK
                         ].astype(o_ref.dtype)
-                else:
+                if not last:
                     acc_out[i] = acc
                     m_out[i : i + 1, :] = m_new
                     l_out[i : i + 1, :] = row_sum
@@ -132,6 +135,76 @@
     return kernel
 
 
+def make_patch(stage, heads, dev_blocks, doc_blk, firsts, groups, head_dim, score_scale):
+    qwidth = groups * head_dim
+
+    def local_index(rel):
+        return rel + stage * dev_blocks - firsts[stage]
+
+    def kernel(rel_ref, q_hbm, kv_ref, acc_hbm, m_hbm, l_hbm, prov_hbm, out_hbm,
+               q_buf, acc_buf, m_buf, l_buf, s_sc, o_f32, o_buf, sems):
+        del prov_hbm
+        for i in range(dev_blocks):
+            regions = stage_regions(stage, i, dev_blocks, doc_blk, firsts)
+            if not regions:
+                continue
+            start = rel_ref[i]
+
+            def patch_block():
+                copies = [
+                    pltpu.make_async_copy(q_hbm.at[pl.ds(i * BLK, BLK)], q_buf, sems.at[0]),
+                    pltpu.make_async_copy(acc_hbm.at[:, i], acc_buf, sems.at[1]),
+                    pltpu.make_async_copy(m_hbm.at[:, pl.ds(i, 1)], m_buf, sems.at[2]),
+                    pltpu.make_async_copy(l_hbm.at[:, pl.ds(i, 1)], l_buf, sems.at[3]),
+                ]
+                for c in copies:
+                    c.start()
+                for c in copies:
+                    c.wait()
+                for h in range(heads):
+                    q = jnp.concatenate(
+                        [q_buf[:, h * qwidth + g * head_dim : h * qwidth + (g + 1) * head_dim] for g in range(groups)],
+                        axis=0,
+                    )
+                    m_blk = None
+                    for r, rels in enumerate(regions):
+                        lo = local_index(rels[0])
+                        k = kv_ref[0, lo * BLK : (lo + len(rels)) * BLK, h * head_dim : (h + 1) * head_dim]
+                        sc = lax.dot_general(
+                            k, q, (((1,), (1,)), ((), ())), preferred_element_type=jnp.float32
+                        ) * score_scale
+                        key = lax.broadcasted_iota(jnp.int32, sc.shape, 0) // BLK + rels[0]
+                        sc = jnp.where(key >= start, sc, -jnp.inf)
+                        s_sc[r, : len(rels) * BLK, :] = sc
+                        mx = jnp.max(sc, axis=0, keepdims=True)
+                        m_blk = mx if m_blk is None else jnp.maximum(m_blk, mx)
+                    m_old = m_buf[h]
+                    m_new = jnp.maximum(m_old, m_blk)
+                    alpha = jnp.exp(m_old - m_new)
+                    row_sum = alpha * l_buf[h]
+                    acc = alpha * acc_buf[h]
+                    for r, rels in enumerate(regions):
+                        p = jnp.exp(s_sc[r, : len(rels) * BLK, :] - m_new)
+                        row_sum = row_sum + jnp.sum(p, axis=0, keepdims=True)
+                        lo = local_index(rels[0])
+                        v = kv_ref[1, lo * BLK : (lo + len(rels)) * BLK, h * head_dim : (h + 1) * head_dim]
+                        acc = acc + lax.dot_general(
+                            v, p.astype(jnp.bfloat16), (((0,), (0,)), ((), ())),
+                            preferred_element_type=jnp.float32,
+                        )
+                    o_f32[h] = jnp.transpose(acc * (1.0 / row_sum))
+                for g in range(groups):
+                    vals = jnp.stack([o_f32[h, g * BLK : (g + 1) * BLK, :] for h in range(heads)], axis=1)
+                    o_buf[:, :, g * head_dim : (g + 1) * head_dim] = vals.astype(o_buf.dtype)
+                out_copy = pltpu.make_async_copy(o_buf, out_hbm.at[pl.ds(i * BLK, BLK)], sems.at[4])
+                out_copy.start()
+                out_copy.wait()
+
+            pl.when(start <= regions[-1][-1])(patch_block)
+
+    return kernel
+
+
 def doc_start_of(doc_blocks, blocks):
     ends = jnp.cumsum(doc_blocks)
     starts = ends - doc_blocks
@@ -184,19 +257,19 @@
 
     state = None
     out = None
-    for stage in range(reach + 1):
+    for stage in range(reach):
         first = stage == 0
-        last = stage == reach
-        kernel = make_stage(stage, first, last, dev_blocks, doc_blk, firsts, groups, head_dim, score_scale)
+        last = False
+        provisional = stage == reach - 1
+        kernel = make_stage(stage, first, last, provisional, dev_blocks, doc_blk, firsts, groups, head_dim, score_scale)
         kv_spec = pl.BlockSpec((2, kv_src[stage].shape[1], head_dim), lambda h, rel: (0, 0, h))
         in_specs = [q_spec, kv_spec] + ([] if first else state_specs)
         args = [rel_start, q2, kv_src[stage]] + ([] if first else list(state))
-        if last:
-            out_shape = jax.ShapeDtypeStruct((tok_rows, heads * qwidth), queries.dtype)
-            out_specs = q_spec
-        else:
-            out_shape = state_shapes
-            out_specs = state_specs
+        out_shape = state_shapes
+        out_specs = state_specs
+        if provisional:
+            out_shape = state_shapes + (jax.ShapeDtypeStruct((tok_rows, heads * qwidth), queries.dtype),)
+            out_specs = state_specs + [q_spec]
         res = pl.pallas_call(
             kernel,
             out_shape=out_shape,
@@ -209,11 +282,42 @@
             ),
             compiler_params=pltpu.CompilerParams(dimension_semantics=("arbitrary",)),
         )(*args)
-        if last:
-            out = res
-        else:
-            state = res
-    return out.reshape(tok_rows, heads, qwidth)
+        state = res[:3]
+        if provisional:
+            out = res[3].reshape(tok_rows, heads, qwidth)
+
+    n_regions = max(1, (dev_blocks + 1) // 2)
+    any_spec = pl.BlockSpec(memory_space=pl.ANY)
+    kv_last = kv_src[reach]
+    out = pl.pallas_call(
+        make_patch(reach, heads, dev_blocks, doc_blk, firsts, groups, head_dim, score_scale),
+        out_shape=jax.ShapeDtypeStruct((tok_rows, heads, qwidth), queries.dtype),
+        grid_spec=pltpu.PrefetchScalarGridSpec(
+            num_scalar_prefetch=1,
+            grid=(1,),
+            in_specs=[
+                any_spec,
+                pl.BlockSpec(kv_last.shape, lambda h, rel: (0, 0, 0)),
+                any_spec,
+                any_spec,
+                any_spec,
+                any_spec,
+            ],
+            out_specs=any_spec,
+            scratch_shapes=[
+                pltpu.VMEM((BLK, heads * qwidth), queries.dtype),
+                pltpu.VMEM((heads, head_dim, rows), jnp.float32),
+                pltpu.VMEM((heads, 1, rows), jnp.float32),
+                pltpu.VMEM((heads, 1, rows), jnp.float32),
+                pltpu.VMEM((n_regions, 2 * BLK, rows), jnp.float32),
+                pltpu.VMEM((heads, rows, head_dim), jnp.float32),
+                pltpu.VMEM((BLK, heads, qwidth), queries.dtype),
+                pltpu.SemaphoreType.DMA((5,)),
+            ],
+        ),
+        input_output_aliases={6: 0},
+    )(rel_start, q2, kv_last, *state, out)
+    return out
 
 
 def solution(mesh):

time: 46 us -> 48.3 us (1.050)
  the two profiles are of different devices: /device:TPU:14 before, /device:TPU:18 now
where the time goes in v7:
time: 48.3 us; the launch traced here: 47.9 us
  Pallas kernels  21.1 us (44%)
  waiting for transfers between devices  11.9 us (25%)
  local copies, waits for them, and re-layouts  7 us (14%)
  starting transfers between devices  6.97 us (14%)
  other arithmetic  0.89 us (2%)
    pallas_call x2, Pallas kernels, on_device(): pl.pallas_call(kernel, out_shape=out_shape, grid_spec=pltpu.PrefetchScala...  13.1 us
    ppermute x2, waiting for transfers between devices, shift_up(): return lax.ppermute(block, axis, [(i, i + 1) for i in range(size - 1)])  11.9 us
    pallas_call x1, Pallas kernels, on_device(): pl.pallas_call(make_patch(reach, heads, dev_blocks, doc_blk, firsts, grou...  7.99 us
    ppermute x2, starting transfers between devices, shift_up(): return lax.ppermute(block, axis, [(i, i + 1) for i in range(size - 1)])  6.97 us
    reshape x1, local copies, waits for them, and re-layouts, on_device(): out = res[3].reshape(tok_rows, heads, qwidth)  2.62 us
    another operation x3, local copies, waits for them, and re-layouts, on_device(): kv_cur = jnp.stack([k2, v2])  2.35 us
    unnamed x12, local copies, waits for them, and re-layouts  2 us
  transfers between devices with their start and end apart: 2, of which 1 were waited for; matrix products, arithmetic and copies ran while one was open for 10% of the time, Pallas kernels for 27%

profile of v7, /device:TPU:18, one launch (start us, length us, event | category | flops | bytes accessed | tf_op | source)
XLA Modules:
  0.0 47.9 jit_solution(10883338052813614770)
XLA Ops:
  0.0 0.0 copy-start.4
  0.0 0.0 copy-start.2
  0.0 1.2 %stack_reshape.6 = bf16[1,512,256]{2,1,0:T(8,128)(2,1)S(1)} reshape(bf16[512,2,128]{2,1,0:T(2,128)(2,1)} %param.5) | data formatting | bytes 524288 | tf_op jit(solution)/shard_map/stack;reshape | solution.py:234
  1.2 1.1 %stack_reshape.7 = bf16[1,512,256]{2,1,0:T(8,128)(2,1)S(1)} reshape(bf16[512,2,128]{2,1,0:T(2,128)(2,1)} %param.6) | data formatting | bytes 524288 | tf_op jit(solution)/shard_map/stack;reshape | solution.py:234
  2.4 0.0 copy-start.1
  2.4 3.5 %collective-permute-start = (bf16[2,512,256]{2,1,0:T(8,128)(2,1)S(1)}, bf16[2,512,256]{2,1,0:T(8,128)(2,1)S(1)}, u32[]{:S(2)}, u32[]{:S(2)}) collective-permute-start(bf16[2,512,256]{2,1,0:T(8,128)(2,1)S(1)} %constant_dynamic-update-slice_fusion.kv_ref), channel_id=1, source_target_pairs={{0,4},{4,8},{8,12},{1,5},{5,9},{9,13},{2,6},{6,10},{10,14},{3,7},{... | collective-permute-start | bytes 1572872 | tf_op jit(solution)/shard_map/ppermute | solution.py:14
  5.9 0.0 copy-done.4
  5.9 0.2 reduce-window.9
  6.1 11.9 %collective-permute-done.kv_ref = bf16[2,512,256]{2,1,0:T(8,128)(2,1)S(1)} collective-permute-done((bf16[2,512,256]{2,1,0:T(8,128)(2,1)S(1)}, bf16[2,512,256]{2,1,0:T(8,128)(2,1)S(1)}, u32[]{:S(2)}, u32[]{:S(2)}) %collective-permute-start) | collective-permute-done | bytes 524320 | tf_op jit(solution)/shard_map/ppermute | solution.py:14
  18.0 0.0 copy-start
  18.0 3.5 %collective-permute-start.1 = (bf16[2,384,256]{2,1,0:T(8,128)(2,1)S(1)}, bf16[2,384,256]{2,1,0:T(8,128)(2,1)S(1)}, u32[]{:S(2)}, u32[]{:S(2)}) collective-permute-start(bf16[2,384,256]{2,1,0:T(8,128)(2,1)S(1)} %slice.4), channel_id=1, source_target_pairs={{0,4},{4,8},{8,12},{1,5},{5,9},{9,13},{2,6},{6,10},{10,14},{3,7},{... | collective-permute-start | bytes 1179656 | tf_op jit(solution)/shard_map/ppermute | solution.py:14
  21.5 0.0 copy-done.2
  21.5 1.2 %copy.6 = bf16[64,8,2,512]{3,1,2,0:T(8,128)(2,1)} copy(bf16[64,8,2,512]{3,2,1,0:T(2,128)(2,1)S(1)} %bitcast.8) | data formatting | bytes 2097152
  22.7 0.2 select_reduce_fusion
  22.9 0.5 %broadcast_subtract_fusion.rel_ref = s32[4]{0:T(128)} fusion(s32[4]{0:T(128)S(1)} %select_reduce_fusion, s32[]{:T(128)S(6)} %mul.3), kind=kLoop, calls=%fused_computation.5 | loop fusion | flops 4 | bytes 36 | tf_op jit(solution)/shard_map/sub | solution.py:228
  23.5 0.0 copy-done.1
  23.5 6.3 %shard_map.46 = (f32[2,4,128,512]{3,2,1,0:T(8,128)}, f32[2,4,512]{2,1,0:T(4,128)}, f32[2,4,512]{2,1,0:T(4,128)}) custom-call(s32[4]{0:T(128)} %broadcast_subtract_fusion.rel_ref, bf16[512,1024]{1,0:T(8,128)(2,1)} %bitcast.5, bf16[2,512,256]{2,1,0:T(8,128)(2,1)} %copy-done.1), custom_call_target="tpu_custom_call" | custom-call | tf_op jit(solution)/shard_map/pallas_call | solution.py:273
  29.7 0.0 copy-done
  29.8 6.8 %shard_map.47 = (f32[2,4,128,512]{3,2,1,0:T(8,128)}, f32[2,4,512]{2,1,0:T(4,128)}, f32[2,4,512]{2,1,0:T(4,128)}, bf16[512,1024]{1,0:T(8,128)(2,1)}) custom-call(s32[4]{0:T(128)} %broadcast_subtract_fusion.rel_ref, bf16[512,1024]{1,0:T(8,128)(2,1)} %bitcast.6, bf16[2,512,256]{2,1,0:T(8,128)(2,1)} %copy-done, f32[2,4,128,512]{3,2,1,0:T(8,128)} %get-tuple-element.12.refs_0_, ...), custom_call_target="tpu_custom_call" | custom-call | tf_op jit(solution)/shard_map/pallas_call | solution.py:273
  36.6 2.6 %reshape.40.prov_hbm = bf16[512,2,512]{2,1,0:T(2,128)(2,1)} reshape(bf16[512,1024]{1,0:T(8,128)(2,1)} %get-tuple-element.18) | data formatting | bytes 2097152 | tf_op jit(solution)/shard_map/reshape | solution.py:287
  39.2 0.0 collective-permute-done.1.kv_ref
  39.2 0.0 copy-start.3
  39.2 0.7 %copy-done.3 = bf16[2,384,256]{2,1,0:T(8,128)(2,1)} copy-done((bf16[2,384,256]{2,1,0:T(8,128)(2,1)}, bf16[2,384,256]{2,1,0:T(8,128)(2,1)S(1)}, u32[]{:S(2)}) %copy-start.3) | copy-done | bytes 393240
  39.9 8.0 %shard_map.48 = bf16[512,2,512]{2,1,0:T(2,128)(2,1)} custom-call(s32[4]{0:T(128)} %broadcast_subtract_fusion.rel_ref, bf16[512,1024]{1,0:T(8,128)(2,1)} %bitcast.7, bf16[2,384,256]{2,1,0:T(8,128)(2,1)} %copy-done.3, f32[2,4,128,512]{3,2,1,0:T(8,128)} %get-tuple-element.15.acc_hbm, ...), custom_call_target="tpu_custom_call", output_to_operand_aliasing={{}: (6, {})} | custom-call | tf_op jit(solution)/shard_map/pallas_call | solution.py:292
  (4 shorter events, 0.1 us)
Async XLA Ops:
  0.0 5.9 %copy-start.4 = (s32[4]{0:T(128)S(1)}, s32[4]{0:T(128)}, u32[]{:S(2)}) copy-start(s32[4]{0:T(128)} %param.7) | copy-start | bytes 52
  0.0 21.5 %copy-start.2 = (bf16[512,2,512]{2,1,0:T(2,128)(2,1)S(1)}, bf16[512,2,512]{2,1,0:T(2,128)(2,1)}, u32[]{:S(2)}) copy-start(bf16[512,2,512]{2,1,0:T(2,128)(2,1)} %param.4) | copy-start | bytes 3145732
  2.4 21.1 %copy-start.1 = (bf16[2,512,256]{2,1,0:T(8,128)(2,1)}, bf16[2,512,256]{2,1,0:T(8,128)(2,1)S(1)}, u32[]{:S(2)}) copy-start(bf16[2,512,256]{2,1,0:T(8,128)(2,1)S(1)} %constant_dynamic-update-slice_fusion.kv_ref) | copy-start | bytes 1572868
  2.4 15.6 %collective-permute-start = (bf16[2,512,256]{2,1,0:T(8,128)(2,1)S(1)}, bf16[2,512,256]{2,1,0:T(8,128)(2,1)S(1)}, u32[]{:S(2)}, u32[]{:S(2)}) collective-permute-start(bf16[2,512,256]{2,1,0:T(8,128)(2,1)S(1)} %constant_dynamic-update-slice_fusion.kv_ref), channel_id=1, source_target_pairs={{0,4},{4,8},{8,12},{1,5},{5,9},{9,13},{2,6},{6,10},{10,14},{3,7},{... | collective-permute-start | bytes 1572872 | tf_op jit(solution)/shard_map/ppermute | solution.py:14
  18.0 11.8 %copy-start = (bf16[2,512,256]{2,1,0:T(8,128)(2,1)}, bf16[2,512,256]{2,1,0:T(8,128)(2,1)S(1)}, u32[]{:S(2)}) copy-start(bf16[2,512,256]{2,1,0:T(8,128)(2,1)S(1)} %collective-permute-done.kv_ref) | copy-start | bytes 1572868
  18.0 21.2 %collective-permute-start.1 = (bf16[2,384,256]{2,1,0:T(8,128)(2,1)S(1)}, bf16[2,384,256]{2,1,0:T(8,128)(2,1)S(1)}, u32[]{:S(2)}, u32[]{:S(2)}) collective-permute-start(bf16[2,384,256]{2,1,0:T(8,128)(2,1)S(1)} %slice.4), channel_id=1, source_target_pairs={{0,4},{4,8},{8,12},{1,5},{5,9},{9,13},{2,6},{6,10},{10,14},{3,7},{... | collective-permute-start | bytes 1179656 | tf_op jit(solution)/shard_map/ppermute | solution.py:14
  39.2 0.7 %copy-start.3 = (bf16[2,384,256]{2,1,0:T(8,128)(2,1)}, bf16[2,384,256]{2,1,0:T(8,128)(2,1)S(1)}, u32[]{:S(2)}) copy-start(bf16[2,384,256]{2,1,0:T(8,128)(2,1)S(1)} %collective-permute-done.1.kv_ref) | copy-start | bytes 1179652

commit v8 on v7

--- a/solution.py
+++ b/solution.py
@@ -141,35 +141,55 @@
     def local_index(rel):
         return rel + stage * dev_blocks - firsts[stage]
 
-    def kernel(rel_ref, q_hbm, kv_ref, acc_hbm, m_hbm, l_hbm, prov_hbm, out_hbm,
-               q_buf, acc_buf, m_buf, l_buf, s_sc, o_f32, o_buf, sems):
+    def kernel(rel_ref, q_hbm, kv_hbm, acc_hbm, m_hbm, l_hbm, prov_hbm, out_hbm,
+               kv_buf, q_buf, acc_buf, m_buf, l_buf, s_sc, o_f32, o_buf, kv_sem, sems):
         del prov_hbm
+        blocks = []
         for i in range(dev_blocks):
             regions = stage_regions(stage, i, dev_blocks, doc_blk, firsts)
-            if not regions:
-                continue
+            if regions:
+                blocks.append((i, regions, rel_ref[i] <= regions[-1][-1]))
+        if not blocks:
+            return
+        any_live = blocks[0][2]
+        for _, _, live in blocks[1:]:
+            any_live = jnp.logical_or(any_live, live)
+        kv_copy = pltpu.make_async_copy(kv_hbm, kv_buf, kv_sem.at[0])
+
+        def block_copies(i):
+            return [
+                pltpu.make_async_copy(q_hbm.at[pl.ds(i * BLK, BLK)], q_buf.at[i], sems.at[i, 0]),
+                pltpu.make_async_copy(acc_hbm.at[:, i], acc_buf.at[i], sems.at[i, 1]),
+                pltpu.make_async_copy(m_hbm.at[:, pl.ds(i, 1)], m_buf.at[i], sems.at[i, 2]),
+                pltpu.make_async_copy(l_hbm.at[:, pl.ds(i, 1)], l_buf.at[i], sems.at[i, 3]),
+            ]
+
+        def out_copy(i):
+            return pltpu.make_async_copy(o_buf.at[i], out_hbm.at[pl.ds(i * BLK, BLK)], sems.at[i, 4])
+
+        pl.when(any_live)(kv_copy.start)
+        for i, _, live in blocks:
+            @pl.when(live)
+            def _():
+                for c in block_copies(i):
+                    c.start()
+        pl.when(any_live)(kv_copy.wait)
+
+        for i, regions, live in blocks:
             start = rel_ref[i]
 
             def patch_block():
-                copies = [
-                    pltpu.make_async_copy(q_hbm.at[pl.ds(i * BLK, BLK)], q_buf, sems.at[0]),
-                    pltpu.make_async_copy(acc_hbm.at[:, i], acc_buf, sems.at[1]),
-                    pltpu.make_async_copy(m_hbm.at[:, pl.ds(i, 1)], m_buf, sems.at[2]),
-                    pltpu.make_async_copy(l_hbm.at[:, pl.ds(i, 1)], l_buf, sems.at[3]),
-                ]
-                for c in copies:
-                    c.start()
-                for c in copies:
+                for c in block_copies(i):
                     c.wait()
                 for h in range(heads):
                     q = jnp.concatenate(
-                        [q_buf[:, h * qwidth + g * head_dim : h * qwidth + (g + 1) * head_dim] for g in range(groups)],
+                        [q_buf[i, :, h * qwidth + g * head_dim : h * qwidth + (g + 1) * head_dim] for g in range(groups)],
                         axis=0,
                     )
                     m_blk = None
                     for r, rels in enumerate(regions):
                         lo = local_index(rels[0])
-                        k = kv_ref[0, lo * BLK : (lo + len(rels)) * BLK, h * head_dim : (h + 1) * head_dim]
+                        k = kv_buf[0, lo * BLK : (lo + len(rels)) * BLK, h * head_dim : (h + 1) * head_dim]
                         sc = lax.dot_general(
                             k, q, (((1,), (1,)), ((), ())), preferred_element_type=jnp.float32
                         ) * score_scale
@@ -178,16 +198,16 @@
                         s_sc[r, : len(rels) * BLK, :] = sc
                         mx = jnp.max(sc, axis=0, keepdims=True)
                         m_blk = mx if m_blk is None else jnp.maximum(m_blk, mx)
-                    m_old = m_buf[h]
+                    m_old = m_buf[i, h]
                     m_new = jnp.maximum(m_old, m_blk)
                     alpha = jnp.exp(m_old - m_new)
-                    row_sum = alpha * l_buf[h]
-                    acc = alpha * acc_buf[h]
+                    row_sum = alpha * l_buf[i, h]
+                    acc = alpha * acc_buf[i, h]
                     for r, rels in enumerate(regions):
                         p = jnp.exp(s_sc[r, : len(rels) * BLK, :] - m_new)
                         row_sum = row_sum + jnp.sum(p, axis=0, keepdims=True)
                         lo = local_index(rels[0])
-                        v = kv_ref[1, lo * BLK : (lo + len(rels)) * BLK, h * head_dim : (h + 1) * head_dim]
+                        v = kv_buf[1, lo * BLK : (lo + len(rels)) * BLK, h * head_dim : (h + 1) * head_dim]
                         acc = acc + lax.dot_general(
                             v, p.astype(jnp.bfloat16), (((0,), (0,)), ((), ())),
                             preferred_element_type=jnp.float32,
@@ -195,12 +215,13 @@
                     o_f32[h] = jnp.transpose(acc * (1.0 / row_sum))
                 for g in range(groups):
                     vals = jnp.stack([o_f32[h, g * BLK : (g + 1) * BLK, :] for h in range(heads)], axis=1)
-                    o_buf[:, :, g * head_dim : (g + 1) * head_dim] = vals.astype(o_buf.dtype)
-                out_copy = pltpu.make_async_copy(o_buf, out_hbm.at[pl.ds(i * BLK, BLK)], sems.at[4])
-                out_copy.start()
-                out_copy.wait()
-
-            pl.when(start <= regions[-1][-1])(patch_block)
+                    o_buf[i, :, :, g * head_dim : (g + 1) * head_dim] = vals.astype(o_buf.dtype)
+                out_copy(i).start()
+
+            pl.when(live)(patch_block)
+
+        for i, _, live in blocks:
+            pl.when(live)(out_copy(i).wait)
 
     return kernel
 
@@ -297,7 +318,7 @@
             grid=(1,),
             in_specs=[
                 any_spec,
-                pl.BlockSpec(kv_last.shape, lambda h, rel: (0, 0, 0)),
+                any_spec,
                 any_spec,
                 any_spec,
                 any_spec,
@@ -305,14 +326,16 @@
             ],
             out_specs=any_spec,
             scratch_shapes=[
-                pltpu.VMEM((BLK, heads * qwidth), queries.dtype),
-                pltpu.VMEM((heads, head_dim, rows), jnp.float32),
-                pltpu.VMEM((heads, 1, rows), jnp.float32),
-                pltpu.VMEM((heads, 1, rows), jnp.float32),
+                pltpu.VMEM(kv_last.shape, kv_last.dtype),
+                pltpu.VMEM((dev_blocks, BLK, heads * qwidth), queries.dtype),
+                pltpu.VMEM((dev_blocks, heads, head_dim, rows), jnp.float32),
+                pltpu.VMEM((dev_blocks, heads, 1, rows), jnp.float32),
+                pltpu.VMEM((dev_blocks, heads, 1, rows), jnp.float32),
                 pltpu.VMEM((n_regions, 2 * BLK, rows), jnp.float32),
                 pltpu.VMEM((heads, rows, head_dim), jnp.float32),
-                pltpu.VMEM((BLK, heads, qwidth), queries.dtype),
-                pltpu.SemaphoreType.DMA((5,)),
+                pltpu.VMEM((dev_blocks, BLK, heads, qwidth), queries.dtype),
+                pltpu.SemaphoreType.DMA((1,)),
+                pltpu.SemaphoreType.DMA((dev_blocks, 5)),
             ],
         ),
         input_output_aliases={6: 0},

time: 48.3 us -> 45.9 us (0.950)
  Pallas kernels: 21.1 us -> 18.8 us
    pallas_call x1, Pallas kernels: 7.99 us -> 5.69 us  [on_device(): pl.pallas_call(make_patch(reach, heads, dev_blocks, doc_blk, firsts, grou...]
  transfers between devices with their start and end apart: 2 -> 2, of which waited for: 1 -> 1; matrix products, arithmetic and copies ran while one was open for 10% -> 10% of each run, Pallas kernels for 27% -> 29%
where the time goes in v8:
time: 45.9 us; the launch traced here: 45.6 us
  Pallas kernels  18.8 us (41%)
  waiting for transfers between devices  11.9 us (26%)
  local copies, waits for them, and re-layouts  7 us (15%)
  starting transfers between devices  6.97 us (15%)
  other arithmetic  0.89 us (2%)
    pallas_call x2, Pallas kernels, on_device(): pl.pallas_call(kernel, out_shape=out_shape, grid_spec=pltpu.PrefetchScala...  13.1 us
    ppermute x2, waiting for transfers between devices, shift_up(): return lax.ppermute(block, axis, [(i, i + 1) for i in range(size - 1)])  11.9 us
    ppermute x2, starting transfers between devices, shift_up(): return lax.ppermute(block, axis, [(i, i + 1) for i in range(size - 1)])  6.97 us
    pallas_call x1, Pallas kernels, on_device(): pl.pallas_call(make_patch(reach, heads, dev_blocks, doc_blk, firsts, grou...  5.69 us
    reshape x1, local copies, waits for them, and re-layouts, on_device(): out = res[3].reshape(tok_rows, heads, qwidth)  2.62 us
    another operation x3, local copies, waits for them, and re-layouts, on_device(): kv_cur = jnp.stack([k2, v2])  2.35 us
    unnamed x12, local copies, waits for them, and re-layouts  2 us
  transfers between devices with their start and end apart: 2, of which 1 were waited for; matrix products, arithmetic and copies ran while one was open for 10% of the time, Pallas kernels for 29%

profile of v8, /device:TPU:18, one launch (start us, length us, event | category | flops | bytes accessed | tf_op | source)
XLA Modules:
  0.0 45.6 jit_solution(8380069000923222301)
XLA Ops:
  0.0 0.0 copy-start.4
  0.0 0.0 copy-start.2
  0.0 1.2 %stack_reshape.6 = bf16[1,512,256]{2,1,0:T(8,128)(2,1)S(1)} reshape(bf16[512,2,128]{2,1,0:T(2,128)(2,1)} %param.5) | data formatting | bytes 524288 | tf_op jit(solution)/shard_map/stack;reshape | solution.py:255
  1.2 1.1 %stack_reshape.7 = bf16[1,512,256]{2,1,0:T(8,128)(2,1)S(1)} reshape(bf16[512,2,128]{2,1,0:T(2,128)(2,1)} %param.6) | data formatting | bytes 524288 | tf_op jit(solution)/shard_map/stack;reshape | solution.py:255
  2.4 0.0 copy-start.1
  2.4 3.5 %collective-permute-start = (bf16[2,512,256]{2,1,0:T(8,128)(2,1)S(1)}, bf16[2,512,256]{2,1,0:T(8,128)(2,1)S(1)}, u32[]{:S(2)}, u32[]{:S(2)}) collective-permute-start(bf16[2,512,256]{2,1,0:T(8,128)(2,1)S(1)} %constant_dynamic-update-slice_fusion.kv_ref), channel_id=1, source_target_pairs={{0,4},{4,8},{8,12},{1,5},{5,9},{9,13},{2,6},{6,10},{10,14},{3,7},{... | collective-permute-start | bytes 1572872 | tf_op jit(solution)/shard_map/ppermute | solution.py:14
  5.9 0.0 copy-done.4
  5.9 0.2 reduce-window.9
  6.1 11.9 %collective-permute-done.kv_ref = bf16[2,512,256]{2,1,0:T(8,128)(2,1)S(1)} collective-permute-done((bf16[2,512,256]{2,1,0:T(8,128)(2,1)S(1)}, bf16[2,512,256]{2,1,0:T(8,128)(2,1)S(1)}, u32[]{:S(2)}, u32[]{:S(2)}) %collective-permute-start) | collective-permute-done | bytes 524320 | tf_op jit(solution)/shard_map/ppermute | solution.py:14
  18.0 0.0 copy-start
  18.0 3.5 %collective-permute-start.1 = (bf16[2,384,256]{2,1,0:T(8,128)(2,1)S(1)}, bf16[2,384,256]{2,1,0:T(8,128)(2,1)S(1)}, u32[]{:S(2)}, u32[]{:S(2)}) collective-permute-start(bf16[2,384,256]{2,1,0:T(8,128)(2,1)S(1)} %slice.4), channel_id=1, source_target_pairs={{0,4},{4,8},{8,12},{1,5},{5,9},{9,13},{2,6},{6,10},{10,14},{3,7},{... | collective-permute-start | bytes 1179656 | tf_op jit(solution)/shard_map/ppermute | solution.py:14
  21.5 0.0 copy-done.2
  21.5 1.2 %copy.6 = bf16[64,8,2,512]{3,1,2,0:T(8,128)(2,1)} copy(bf16[64,8,2,512]{3,2,1,0:T(2,128)(2,1)S(1)} %bitcast.8) | data formatting | bytes 2097152
  22.7 0.2 select_reduce_fusion
  22.9 0.5 %broadcast_subtract_fusion.rel_ref = s32[4]{0:T(128)} fusion(s32[4]{0:T(128)S(1)} %select_reduce_fusion, s32[]{:T(128)S(6)} %mul.3), kind=kLoop, calls=%fused_computation.5 | loop fusion | flops 4 | bytes 36 | tf_op jit(solution)/shard_map/sub | solution.py:249
  23.5 0.0 copy-done.1
  23.5 6.3 %shard_map.46 = (f32[2,4,128,512]{3,2,1,0:T(8,128)}, f32[2,4,512]{2,1,0:T(4,128)}, f32[2,4,512]{2,1,0:T(4,128)}) custom-call(s32[4]{0:T(128)} %broadcast_subtract_fusion.rel_ref, bf16[512,1024]{1,0:T(8,128)(2,1)} %bitcast.5, bf16[2,512,256]{2,1,0:T(8,128)(2,1)} %copy-done.1), custom_call_target="tpu_custom_call" | custom-call | tf_op jit(solution)/shard_map/pallas_call | solution.py:294
  29.7 0.0 copy-done
  29.8 6.8 %shard_map.47 = (f32[2,4,128,512]{3,2,1,0:T(8,128)}, f32[2,4,512]{2,1,0:T(4,128)}, f32[2,4,512]{2,1,0:T(4,128)}, bf16[512,1024]{1,0:T(8,128)(2,1)}) custom-call(s32[4]{0:T(128)} %broadcast_subtract_fusion.rel_ref, bf16[512,1024]{1,0:T(8,128)(2,1)} %bitcast.6, bf16[2,512,256]{2,1,0:T(8,128)(2,1)} %copy-done, f32[2,4,128,512]{3,2,1,0:T(8,128)} %get-tuple-element.12.refs_0_, ...), custom_call_target="tpu_custom_call" | custom-call | tf_op jit(solution)/shard_map/pallas_call | solution.py:294
  36.6 2.6 %reshape.40.prov_hbm = bf16[512,2,512]{2,1,0:T(2,128)(2,1)} reshape(bf16[512,1024]{1,0:T(8,128)(2,1)} %get-tuple-element.18) | data formatting | bytes 2097152 | tf_op jit(solution)/shard_map/reshape | solution.py:308
  39.2 0.0 collective-permute-done.1.kv_hbm
  39.2 0.0 copy-start.3
  39.2 0.7 %copy-done.3 = bf16[2,384,256]{2,1,0:T(8,128)(2,1)} copy-done((bf16[2,384,256]{2,1,0:T(8,128)(2,1)}, bf16[2,384,256]{2,1,0:T(8,128)(2,1)S(1)}, u32[]{:S(2)}) %copy-start.3) | copy-done | bytes 393240
  39.9 5.7 %shard_map.48 = bf16[512,2,512]{2,1,0:T(2,128)(2,1)} custom-call(s32[4]{0:T(128)} %broadcast_subtract_fusion.rel_ref, bf16[512,1024]{1,0:T(8,128)(2,1)} %bitcast.7, bf16[2,384,256]{2,1,0:T(8,128)(2,1)} %copy-done.3, f32[2,4,128,512]{3,2,1,0:T(8,128)} %get-tuple-element.15.acc_hbm, ...), custom_call_target="tpu_custom_call", output_to_operand_aliasing={{}: (6, {})} | custom-call | tf_op jit(solution)/shard_map/pallas_call | solution.py:313
  (4 shorter events, 0.1 us)
Async XLA Ops:
  0.0 5.9 %copy-start.4 = (s32[4]{0:T(128)S(1)}, s32[4]{0:T(128)}, u32[]{:S(2)}) copy-start(s32[4]{0:T(128)} %param.7) | copy-start | bytes 52
  0.0 21.5 %copy-start.2 = (bf16[512,2,512]{2,1,0:T(2,128)(2,1)S(1)}, bf16[512,2,512]{2,1,0:T(2,128)(2,1)}, u32[]{:S(2)}) copy-start(bf16[512,2,512]{2,1,0:T(2,128)(2,1)} %param.4) | copy-start | bytes 3145732
  2.4 21.1 %copy-start.1 = (bf16[2,512,256]{2,1,0:T(8,128)(2,1)}, bf16[2,512,256]{2,1,0:T(8,128)(2,1)S(1)}, u32[]{:S(2)}) copy-start(bf16[2,512,256]{2,1,0:T(8,128)(2,1)S(1)} %constant_dynamic-update-slice_fusion.kv_ref) | copy-start | bytes 1572868
  2.4 15.6 %collective-permute-start = (bf16[2,512,256]{2,1,0:T(8,128)(2,1)S(1)}, bf16[2,512,256]{2,1,0:T(8,128)(2,1)S(1)}, u32[]{:S(2)}, u32[]{:S(2)}) collective-permute-start(bf16[2,512,256]{2,1,0:T(8,128)(2,1)S(1)} %constant_dynamic-update-slice_fusion.kv_ref), channel_id=1, source_target_pairs={{0,4},{4,8},{8,12},{1,5},{5,9},{9,13},{2,6},{6,10},{10,14},{3,7},{... | collective-permute-start | bytes 1572872 | tf_op jit(solution)/shard_map/ppermute | solution.py:14
  18.0 11.8 %copy-start = (bf16[2,512,256]{2,1,0:T(8,128)(2,1)}, bf16[2,512,256]{2,1,0:T(8,128)(2,1)S(1)}, u32[]{:S(2)}) copy-start(bf16[2,512,256]{2,1,0:T(8,128)(2,1)S(1)} %collective-permute-done.kv_ref) | copy-start | bytes 1572868
  18.0 21.2 %collective-permute-start.1 = (bf16[2,384,256]{2,1,0:T(8,128)(2,1)S(1)}, bf16[2,384,256]{2,1,0:T(8,128)(2,1)S(1)}, u32[]{:S(2)}, u32[]{:S(2)}) collective-permute-start(bf16[2,384,256]{2,1,0:T(8,128)(2,1)S(1)} %slice.4), channel_id=1, source_target_pairs={{0,4},{4,8},{8,12},{1,5},{5,9},{9,13},{2,6},{6,10},{10,14},{3,7},{... | collective-permute-start | bytes 1179656 | tf_op jit(solution)/shard_map/ppermute | solution.py:14
  39.2 0.7 %copy-start.3 = (bf16[2,384,256]{2,1,0:T(8,128)(2,1)}, bf16[2,384,256]{2,1,0:T(8,128)(2,1)S(1)}, u32[]{:S(2)}) copy-start(bf16[2,384,256]{2,1,0:T(8,128)(2,1)S(1)} %collective-permute-done.1.kv_hbm) | copy-start | bytes 1179652

commit v9 on v8

--- a/solution.py
+++ b/solution.py
@@ -252,14 +252,15 @@
     k2 = keys.reshape(tok_rows, heads * head_dim)
     v2 = values.reshape(tok_rows, heads * head_dim)
 
-    kv_cur = jnp.stack([k2, v2])
-    kv_src = [kv_cur]
+    kv_src = [jnp.stack([k2, v2])]
+    k_cur, v_cur = keys, values
     prev_first = 0
     for r in range(1, reach + 1):
         cut = (firsts[r] - prev_first) * BLK
-        kv_cur = shift_up(kv_cur[:, cut:], "seq")
+        k_cur, v_cur = shift_up((k_cur[cut:], v_cur[cut:]), "seq")
         prev_first = firsts[r]
-        kv_src.append(kv_cur)
+        n = k_cur.shape[0]
+        kv_src.append(jnp.stack([k_cur.reshape(n, heads * head_dim), v_cur.reshape(n, heads * head_dim)]))
 
     state_shapes = (
         jax.ShapeDtypeStruct((heads, dev_blocks, head_dim, rows), jnp.float32),

time: 45.9 us -> 44.8 us (0.976)
  the two profiles are of different devices: /device:TPU:18 before, /device:TPU:16 now
where the time goes in v9:
time: 44.8 us; the launch traced here: 44.4 us
  Pallas kernels  18.8 us (42%)
  starting transfers between devices  11.8 us (26%)
  local copies, waits for them, and re-layouts  8.17 us (18%)
  other arithmetic  4.72 us (11%)
  waiting for transfers between devices  0.86 us (2%)
    pallas_call x2, Pallas kernels, on_device(): pl.pallas_call(kernel, out_shape=out_shape, grid_spec=pltpu.PrefetchScala...  13.1 us
    ppermute x4, starting transfers between devices, shift_up(): return lax.ppermute(block, axis, [(i, i + 1) for i in range(size - 1)])  11.8 us
    pallas_call x1, Pallas kernels, on_device(): pl.pallas_call(make_patch(reach, heads, dev_blocks, doc_blk, firsts, grou...  5.69 us
    reshape x1, local copies, waits for them, and re-layouts, on_device(): out = res[3].reshape(tok_rows, heads, qwidth)  2.62 us
    unnamed x1, local copies, waits for them, and re-layouts  2.44 us
    another operation x2, local copies, waits for them, and re-layouts, on_device(): kv_src = [jnp.stack([k2, v2])]  2.24 us
    another operation x2, other arithmetic, on_device(): jnp.stack([k_cur.reshape(n, heads * head_dim), v_cur.reshape(n, heads * h...  1.63 us
  transfers between devices with their start and end apart: 4, of which 1 were waited for; matrix products, arithmetic and copies ran while one was open for 27% of the time, Pallas kernels for 29%

profile of v9, /device:TPU:16, one launch (start us, length us, event | category | flops | bytes accessed | tf_op | source)
XLA Modules:
  0.0 44.4 jit_solution(11947274519672494876)
XLA Ops:
  0.0 3.5 %collective-permute-start = (bf16[512,2,128]{2,1,0:T(2,128)(2,1)}, bf16[512,2,128]{2,1,0:T(2,128)(2,1)S(1)}, u32[]{:S(2)}, u32[]{:S(2)}) collective-permute-start(bf16[512,2,128]{2,1,0:T(2,128)(2,1)} %param.5), channel_id=1, source_target_pairs={{0,4},{4,8},{8,12},{1,5},{5,9},{9,13},{2,6},{6,10},{10,14},{3,7},{... | collective-permute-start | bytes 786440 | tf_op jit(solution)/shard_map/ppermute | solution.py:14
  3.5 1.9 %collective-permute-start.2 = (bf16[512,2,128]{2,1,0:T(2,128)(2,1)}, bf16[512,2,128]{2,1,0:T(2,128)(2,1)S(1)}, u32[]{:S(2)}, u32[]{:S(2)}) collective-permute-start(bf16[512,2,128]{2,1,0:T(2,128)(2,1)} %param.6), channel_id=1, source_target_pairs={{0,4},{4,8},{8,12},{1,5},{5,9},{9,13},{2,6},{6,10},{10,14},{3,7},{... | collective-permute-start | bytes 786440 | tf_op jit(solution)/shard_map/ppermute | solution.py:14
  5.4 0.8 %reduce-window.9 = s32[4,1]{0,1:T(1,128)S(1)} reduce-window(s32[4,1]{0,1:T(1,128)} %bitcast.9, s32[]{:T(128)} %constant.4.clone.1), window={size=4x1 pad=3_0x0_0}, to_apply=%region_0.0 | reduce-window | flops 12 | bytes 36 | tf_op jit(solution)/shard_map/reduce-window.4
  6.2 0.7 %bitcast_subtract_fusion = (s32[4]{0:T(128)S(1)}, s32[4]{0:T(128)S(1)}) fusion(s32[4]{0:T(128)} %param.7, s32[4,1]{0,1:T(1,128)S(1)} %reduce-window.9, s32[]{:T(128)S(6)} %mul.3), kind=kLoop, calls=%fused_computation.4 | loop fusion | flops 8 | bytes 68 | tf_op jit(solution)/shard_map/sub | solution.py:231
  6.9 0.2 select_reduce_fusion
  7.1 1.1 %stack_reshape.22 = bf16[1,512,256]{2,1,0:T(8,128)(2,1)S(1)} reshape(bf16[512,2,128]{2,1,0:T(2,128)(2,1)} %param.5) | data formatting | bytes 524288 | tf_op jit(solution)/shard_map/stack;reshape | solution.py:255
  8.2 1.1 %stack_reshape.23 = bf16[1,512,256]{2,1,0:T(8,128)(2,1)S(1)} reshape(bf16[512,2,128]{2,1,0:T(2,128)(2,1)} %param.6) | data formatting | bytes 524288 | tf_op jit(solution)/shard_map/stack;reshape | solution.py:255
  9.3 2.4 %copy.6 = bf16[64,8,2,512]{3,1,2,0:T(8,128)(2,1)} copy(bf16[64,8,2,512]{3,2,1,0:T(2,128)(2,1)} %bitcast.8) | data formatting | bytes 2097152
  11.8 0.6 %broadcast_subtract_fusion.rel_ref = s32[4]{0:T(128)} fusion(s32[4]{0:T(128)S(1)} %select_reduce_fusion, s32[]{:T(128)S(6)} %mul.3), kind=kLoop, calls=%fused_computation.6 | loop fusion | flops 4 | bytes 36 | tf_op jit(solution)/shard_map/sub | solution.py:249
  12.4 0.1 slice.8
  12.5 2.4 %collective-permute-start.1 = (bf16[384,2,128]{2,1,0:T(2,128)(2,1)S(1)}, bf16[384,2,128]{2,1,0:T(2,128)(2,1)S(1)}, u32[]{:S(2)}, u32[]{:S(2)}) collective-permute-start(bf16[384,2,128]{2,1,0:T(2,128)(2,1)S(1)} %slice.8), channel_id=1, source_target_pairs={{0,4},{4,8},{8,12},{1,5},{5,9},{9,13},{2,6},{6,10},{10,14},{3,7},{... | collective-permute-start | bytes 589832 | tf_op jit(solution)/shard_map/ppermute | solution.py:14
  14.9 0.9 %collective-permute-done.2 = bf16[512,2,128]{2,1,0:T(2,128)(2,1)S(1)} collective-permute-done((bf16[512,2,128]{2,1,0:T(2,128)(2,1)}, bf16[512,2,128]{2,1,0:T(2,128)(2,1)S(1)}, u32[]{:S(2)}, u32[]{:S(2)}) %collective-permute-start.2) | collective-permute-done | bytes 262176 | tf_op jit(solution)/shard_map/ppermute | solution.py:14
  15.8 0.1 slice.9
  15.9 4.0 %collective-permute-start.3 = (bf16[384,2,128]{2,1,0:T(2,128)(2,1)S(1)}, bf16[384,2,128]{2,1,0:T(2,128)(2,1)S(1)}, u32[]{:S(2)}, u32[]{:S(2)}) collective-permute-start(bf16[384,2,128]{2,1,0:T(2,128)(2,1)S(1)} %slice.9), channel_id=1, source_target_pairs={{0,4},{4,8},{8,12},{1,5},{5,9},{9,13},{2,6},{6,10},{10,14},{3,7},{... | collective-permute-start | bytes 589832 | tf_op jit(solution)/shard_map/ppermute | solution.py:14
  19.9 0.8 %pad_maximum_fusion.1.kv_ref = bf16[2,512,256]{2,1,0:T(8,128)(2,1)} fusion(bf16[1,512,256]{2,1,0:T(8,128)(2,1)S(1)} %stack_reshape.23, bf16[1,512,256]{2,1,0:T(8,128)(2,1)S(1)} %stack_reshape.22), kind=kLoop, calls=%fused_computation.1 | loop fusion | flops 262144 | bytes 1048576 | tf_op jit(solution)/shard_map/stack | solution.py:255
  20.7 6.3 %shard_map.46 = (f32[2,4,128,512]{3,2,1,0:T(8,128)}, f32[2,4,512]{2,1,0:T(4,128)}, f32[2,4,512]{2,1,0:T(4,128)}) custom-call(s32[4]{0:T(128)} %broadcast_subtract_fusion.rel_ref, bf16[512,1024]{1,0:T(8,128)(2,1)} %bitcast.5, bf16[2,512,256]{2,1,0:T(8,128)(2,1)} %pad_maximum_fusion.1.kv_ref), custom_call_target="tpu_custom_call" | custom-call | tf_op jit(solution)/shard_map/pallas_call | solution.py:295
  27.0 0.2 stack_reshape.20
  27.2 0.2 stack_reshape.21
  27.4 0.8 %pad_maximum_fusion.kv_ref = bf16[2,512,256]{2,1,0:T(8,128)(2,1)} fusion(bf16[1,512,256]{2,1,0:T(8,128)(2,1)S(1)} %stack_reshape.21, bf16[1,512,256]{2,1,0:T(8,128)(2,1)S(1)} %stack_reshape.20), kind=kLoop, calls=%fused_computation | loop fusion | flops 262144 | bytes 1048576 | tf_op jit(solution)/shard_map/stack | solution.py:263
  28.2 6.8 %shard_map.47 = (f32[2,4,128,512]{3,2,1,0:T(8,128)}, f32[2,4,512]{2,1,0:T(4,128)}, f32[2,4,512]{2,1,0:T(4,128)}, bf16[512,1024]{1,0:T(8,128)(2,1)}) custom-call(s32[4]{0:T(128)} %broadcast_subtract_fusion.rel_ref, bf16[512,1024]{1,0:T(8,128)(2,1)} %bitcast.6, bf16[2,512,256]{2,1,0:T(8,128)(2,1)} %pad_maximum_fusion.kv_ref, ...), custom_call_target="tpu_custom_call" | custom-call | tf_op jit(solution)/shard_map/pallas_call | solution.py:295
  35.0 2.6 %reshape.40.prov_hbm = bf16[512,2,512]{2,1,0:T(2,128)(2,1)} reshape(bf16[512,1024]{1,0:T(8,128)(2,1)} %get-tuple-element.18) | data formatting | bytes 2097152 | tf_op jit(solution)/shard_map/reshape | solution.py:309
  37.8 0.1 stack_reshape.19
  37.9 0.8 %pad_maximum_fusion.2.kv_hbm = bf16[2,384,256]{2,1,0:T(8,128)(2,1)} fusion(bf16[1,384,256]{2,1,0:T(8,128)(2,1)S(1)} %stack_reshape.19, bf16[1,384,256]{2,1,0:T(8,128)(2,1)S(1)} %stack_reshape.18), kind=kLoop, calls=%fused_computation.2 | loop fusion | flops 196608 | bytes 786432 | tf_op jit(solution)/shard_map/stack | solution.py:263
  38.7 5.7 %shard_map.48 = bf16[512,2,512]{2,1,0:T(2,128)(2,1)} custom-call(s32[4]{0:T(128)} %broadcast_subtract_fusion.rel_ref, bf16[512,1024]{1,0:T(8,128)(2,1)} %bitcast.7, bf16[2,384,256]{2,1,0:T(8,128)(2,1)} %pad_maximum_fusion.2.kv_hbm, f32[2,4,128,512]{3,2,1,0:T(8,128)} %get-tuple-element.15.acc_hbm, ...), custom_call_target="tpu_custom_call", output_to_operand_aliasing={{}: (6, {})} | custom-call | tf_op jit(solution)/shard_map/pallas_call | solution.py:314
  (4 shorter events, 0.1 us)
Async XLA Ops:
  0.0 12.4 %collective-permute-start = (bf16[512,2,128]{2,1,0:T(2,128)(2,1)}, bf16[512,2,128]{2,1,0:T(2,128)(2,1)S(1)}, u32[]{:S(2)}, u32[]{:S(2)}) collective-permute-start(bf16[512,2,128]{2,1,0:T(2,128)(2,1)} %param.5), channel_id=1, source_target_pairs={{0,4},{4,8},{8,12},{1,5},{5,9},{9,13},{2,6},{6,10},{10,14},{3,7},{... | collective-permute-start | bytes 786440 | tf_op jit(solution)/shard_map/ppermute | solution.py:14
  3.5 12.3 %collective-permute-start.2 = (bf16[512,2,128]{2,1,0:T(2,128)(2,1)}, bf16[512,2,128]{2,1,0:T(2,128)(2,1)S(1)}, u32[]{:S(2)}, u32[]{:S(2)}) collective-permute-start(bf16[512,2,128]{2,1,0:T(2,128)(2,1)} %param.6), channel_id=1, source_target_pairs={{0,4},{4,8},{8,12},{1,5},{5,9},{9,13},{2,6},{6,10},{10,14},{3,7},{... | collective-permute-start | bytes 786440 | tf_op jit(solution)/shard_map/ppermute | solution.py:14
  12.5 25.1 %collective-permute-start.1 = (bf16[384,2,128]{2,1,0:T(2,128)(2,1)S(1)}, bf16[384,2,128]{2,1,0:T(2,128)(2,1)S(1)}, u32[]{:S(2)}, u32[]{:S(2)}) collective-permute-start(bf16[384,2,128]{2,1,0:T(2,128)(2,1)S(1)} %slice.8), channel_id=1, source_target_pairs={{0,4},{4,8},{8,12},{1,5},{5,9},{9,13},{2,6},{6,10},{10,14},{3,7},{... | collective-permute-start | bytes 589832 | tf_op jit(solution)/shard_map/ppermute | solution.py:14
  15.9 21.9 %collective-permute-start.3 = (bf16[384,2,128]{2,1,0:T(2,128)(2,1)S(1)}, bf16[384,2,128]{2,1,0:T(2,128)(2,1)S(1)}, u32[]{:S(2)}, u32[]{:S(2)}) collective-permute-start(bf16[384,2,128]{2,1,0:T(2,128)(2,1)S(1)} %slice.9), channel_id=1, source_target_pairs={{0,4},{4,8},{8,12},{1,5},{5,9},{9,13},{2,6},{6,10},{10,14},{3,7},{... | collective-permute-start | bytes 589832 | tf_op jit(solution)/shard_map/ppermute | solution.py:14

commit v10 on v9

--- a/solution.py
+++ b/solution.py
@@ -253,14 +253,17 @@
     v2 = values.reshape(tok_rows, heads * head_dim)
 
     kv_src = [jnp.stack([k2, v2])]
-    k_cur, v_cur = keys, values
+    kv_cur = jnp.concatenate([keys, values], axis=1)
     prev_first = 0
     for r in range(1, reach + 1):
         cut = (firsts[r] - prev_first) * BLK
-        k_cur, v_cur = shift_up((k_cur[cut:], v_cur[cut:]), "seq")
+        kv_cur = shift_up(kv_cur[cut:], "seq")
         prev_first = firsts[r]
-        n = k_cur.shape[0]
-        kv_src.append(jnp.stack([k_cur.reshape(n, heads * head_dim), v_cur.reshape(n, heads * head_dim)]))
+        n = kv_cur.shape[0]
+        kv_src.append(jnp.stack([
+            kv_cur[:, :heads].reshape(n, heads * head_dim),
+            kv_cur[:, heads:].reshape(n, heads * head_dim),
+        ]))
 
     state_shapes = (
         jax.ShapeDtypeStruct((heads, dev_blocks, head_dim, rows), jnp.float32),

time: 44.8 us -> 47.5 us (1.060)
  waiting for transfers between devices: 0.86 us -> 8.94 us
  starting transfers between devices: 11.8 us -> 6.97 us
  local copies, waits for them, and re-layouts: 8.17 us -> 7.47 us
    ppermute x4 -> x2, waiting for transfers between devices: 0.86 us -> 8.94 us  [shift_up(): return lax.ppermute(block, axis, [(i, i + 1) for i in range(size - 1)])]
    ppermute x4 -> x2, starting transfers between devices: 11.8 us -> 6.97 us  [shift_up(): return lax.ppermute(block, axis, [(i, i + 1) for i in range(size - 1)])]
    concatenate x0 -> x1, other arithmetic: none -> 1.66 us  [on_device(): kv_cur = jnp.concatenate([keys, values], axis=1)]
    unnamed x1 -> x5, local copies, waits for them, and re-layouts: 2.44 us -> 1.23 us
    another operation x3, other arithmetic: 2.46 us -> 1.8 us  [the longest x2 1.62 us: on_device(): jnp.stack([kv_cur[:, :heads].reshape(n, heads * head_dim), kv_cur[:, head...]
    sub x1, other arithmetic: 0.66 us -> 0.01 us  [doc_start_of(): starts = ends - doc_blocks]
    slice x2 -> x3, local copies, waits for them, and re-layouts: 0.27 us -> 0.78 us  [the longest x2 0.64 us: on_device(): kv_cur[:, :heads].reshape(n, heads * head_dim)]
  transfers between devices with their start and end apart: 4 -> 2, of which waited for: 1 -> 1; matrix products, arithmetic and copies ran while one was open for 27% -> 20% of each run, Pallas kernels for 29% -> 28%
where the time goes in v10:
time: 47.5 us; the launch traced here: 47.2 us
  Pallas kernels  18.8 us (40%)
  waiting for transfers between devices  8.94 us (19%)
  local copies, waits for them, and re-layouts  7.47 us (16%)
  starting transfers between devices  6.97 us (15%)
  other arithmetic  4.98 us (10%)
    pallas_call x2, Pallas kernels, on_device(): pl.pallas_call(kernel, out_shape=out_shape, grid_spec=pltpu.PrefetchScala...  13.1 us
    ppermute x2, waiting for transfers between devices, shift_up(): return lax.ppermute(block, axis, [(i, i + 1) for i in range(size - 1)])  8.94 us
    ppermute x2, starting transfers between devices, shift_up(): return lax.ppermute(block, axis, [(i, i + 1) for i in range(size - 1)])  6.97 us
    pallas_call x1, Pallas kernels, on_device(): pl.pallas_call(make_patch(reach, heads, dev_blocks, doc_blk, firsts, grou...  5.69 us
    reshape x1, local copies, waits for them, and re-layouts, on_device(): out = res[3].reshape(tok_rows, heads, qwidth)  2.62 us
    another operation x2, local copies, waits for them, and re-layouts, on_device(): kv_src = [jnp.stack([k2, v2])]  2.24 us
    concatenate x1, other arithmetic, on_device(): kv_cur = jnp.concatenate([keys, values], axis=1)  1.66 us
    another operation x2, other arithmetic, on_device(): jnp.stack([kv_cur[:, :heads].reshape(n, heads * head_dim), kv_cur[:, head...  1.62 us
  transfers between devices with their start and end apart: 2, of which 1 were waited for; matrix products, arithmetic and copies ran while one was open for 20% of the time, Pallas kernels for 28%

profile of v10, /device:TPU:16, one launch (start us, length us, event | category | flops | bytes accessed | tf_op | source)
XLA Modules:
  0.0 47.2 jit_solution(7079247447601508164)
XLA Ops:
  0.0 1.7 %pad_maximum_fusion = bf16[512,4,128]{2,1,0:T(4,128)(2,1)S(1)} fusion(bf16[512,2,128]{2,1,0:T(2,128)(2,1)} %param.6, bf16[512,2,128]{2,1,0:T(2,128)(2,1)} %param.5), kind=kLoop, calls=%fused_computation | loop fusion | flops 1048576 | bytes 1048576 | tf_op jit(solution)/shard_map/concatenate | solution.py:256
  1.7 3.5 %collective-permute-start = (bf16[512,4,128]{2,1,0:T(4,128)(2,1)S(1)}, bf16[512,4,128]{2,1,0:T(4,128)(2,1)S(1)}, u32[]{:S(2)}, u32[]{:S(2)}) collective-permute-start(bf16[512,4,128]{2,1,0:T(4,128)(2,1)S(1)} %pad_maximum_fusion), channel_id=1, source_target_pairs={{0,4},{4,8},{8,12},{1,5},{5,9},{9,13},{2,6},{6,10},{10,14},{3,7},{... | collective-permute-start | bytes 1572872 | tf_op jit(solution)/shard_map/ppermute | solution.py:14
  5.2 1.1 %stack_reshape.22 = bf16[1,512,256]{2,1,0:T(8,128)(2,1)S(1)} reshape(bf16[512,2,128]{2,1,0:T(2,128)(2,1)} %param.5) | data formatting | bytes 524288 | tf_op jit(solution)/shard_map/stack;reshape | solution.py:255
  6.3 1.1 %stack_reshape.23 = bf16[1,512,256]{2,1,0:T(8,128)(2,1)S(1)} reshape(bf16[512,2,128]{2,1,0:T(2,128)(2,1)} %param.6) | data formatting | bytes 524288 | tf_op jit(solution)/shard_map/stack;reshape | solution.py:255
  7.4 0.2 reduce-window.9
  7.6 0.2 select_reduce_fusion
  7.8 0.5 %broadcast_subtract_fusion.rel_ref = s32[4]{0:T(128)} fusion(s32[4]{0:T(128)S(1)} %select_reduce_fusion, s32[]{:T(128)S(6)} %mul.3), kind=kLoop, calls=%fused_computation.7 | loop fusion | flops 4 | bytes 36 | tf_op jit(solution)/shard_map/sub | solution.py:249
  8.3 8.9 %collective-permute-done = bf16[512,4,128]{2,1,0:T(4,128)(2,1)S(1)} collective-permute-done((bf16[512,4,128]{2,1,0:T(4,128)(2,1)S(1)}, bf16[512,4,128]{2,1,0:T(4,128)(2,1)S(1)}, u32[]{:S(2)}, u32[]{:S(2)}) %collective-permute-start) | collective-permute-done | bytes 524320 | tf_op jit(solution)/shard_map/ppermute | solution.py:14
  17.2 0.1 slice.20
  17.4 3.5 %collective-permute-start.1 = (bf16[384,4,128]{2,1,0:T(4,128)(2,1)S(1)}, bf16[384,4,128]{2,1,0:T(4,128)(2,1)S(1)}, u32[]{:S(2)}, u32[]{:S(2)}) collective-permute-start(bf16[384,4,128]{2,1,0:T(4,128)(2,1)S(1)} %slice.20), channel_id=1, source_target_pairs={{0,4},{4,8},{8,12},{1,5},{5,9},{9,13},{2,6},{6,10},{10,14},{3,7},{... | collective-permute-start | bytes 1179656 | tf_op jit(solution)/shard_map/ppermute | solution.py:14
  20.9 0.8 %pad_maximum_fusion.2.kv_ref = bf16[2,512,256]{2,1,0:T(8,128)(2,1)} fusion(bf16[1,512,256]{2,1,0:T(8,128)(2,1)S(1)} %stack_reshape.23, bf16[1,512,256]{2,1,0:T(8,128)(2,1)S(1)} %stack_reshape.22), kind=kLoop, calls=%fused_computation.2 | loop fusion | flops 262144 | bytes 1048576 | tf_op jit(solution)/shard_map/stack | solution.py:255
  21.7 1.2 %copy.6 = bf16[64,8,2,512]{3,1,2,0:T(8,128)(2,1)} copy(bf16[64,8,2,512]{3,2,1,0:T(2,128)(2,1)S(1)} %bitcast.8) | data formatting | bytes 2097152
  22.9 6.3 %shard_map.46 = (f32[2,4,128,512]{3,2,1,0:T(8,128)}, f32[2,4,512]{2,1,0:T(4,128)}, f32[2,4,512]{2,1,0:T(4,128)}) custom-call(s32[4]{0:T(128)} %broadcast_subtract_fusion.rel_ref, bf16[512,1024]{1,0:T(8,128)(2,1)} %bitcast.5, bf16[2,512,256]{2,1,0:T(8,128)(2,1)} %pad_maximum_fusion.2.kv_ref), custom_call_target="tpu_custom_call" | custom-call | tf_op jit(solution)/shard_map/pallas_call | solution.py:298
  29.2 0.4 fusion
  29.6 0.2 stack_reshape.20
  29.8 0.2 stack_reshape.21
  29.9 0.8 %pad_maximum_fusion.1.kv_ref = bf16[2,512,256]{2,1,0:T(8,128)(2,1)} fusion(bf16[1,512,256]{2,1,0:T(8,128)(2,1)S(1)} %stack_reshape.21, bf16[1,512,256]{2,1,0:T(8,128)(2,1)S(1)} %stack_reshape.20), kind=kLoop, calls=%fused_computation.1 | loop fusion | flops 262144 | bytes 1048576 | tf_op jit(solution)/shard_map/stack | solution.py:263
  30.8 6.8 %shard_map.47 = (f32[2,4,128,512]{3,2,1,0:T(8,128)}, f32[2,4,512]{2,1,0:T(4,128)}, f32[2,4,512]{2,1,0:T(4,128)}, bf16[512,1024]{1,0:T(8,128)(2,1)}) custom-call(s32[4]{0:T(128)} %broadcast_subtract_fusion.rel_ref, bf16[512,1024]{1,0:T(8,128)(2,1)} %bitcast.6, bf16[2,512,256]{2,1,0:T(8,128)(2,1)} %pad_maximum_fusion.1.kv_ref, ...), custom_call_target="tpu_custom_call" | custom-call | tf_op jit(solution)/shard_map/pallas_call | solution.py:298
  37.6 2.6 %reshape.40.prov_hbm = bf16[512,2,512]{2,1,0:T(2,128)(2,1)} reshape(bf16[512,1024]{1,0:T(8,128)(2,1)} %get-tuple-element.18) | data formatting | bytes 2097152 | tf_op jit(solution)/shard_map/reshape | solution.py:312
  40.2 0.3 fusion.1
  40.5 0.1 stack_reshape.18
  40.6 0.1 stack_reshape.19
  40.8 0.8 %pad_maximum_fusion.3.kv_hbm = bf16[2,384,256]{2,1,0:T(8,128)(2,1)} fusion(bf16[1,384,256]{2,1,0:T(8,128)(2,1)S(1)} %stack_reshape.19, bf16[1,384,256]{2,1,0:T(8,128)(2,1)S(1)} %stack_reshape.18), kind=kLoop, calls=%fused_computation.3 | loop fusion | flops 196608 | bytes 786432 | tf_op jit(solution)/shard_map/stack | solution.py:263
  41.5 5.7 %shard_map.48 = bf16[512,2,512]{2,1,0:T(2,128)(2,1)} custom-call(s32[4]{0:T(128)} %broadcast_subtract_fusion.rel_ref, bf16[512,1024]{1,0:T(8,128)(2,1)} %bitcast.7, bf16[2,384,256]{2,1,0:T(8,128)(2,1)} %pad_maximum_fusion.3.kv_hbm, f32[2,4,128,512]{3,2,1,0:T(8,128)} %get-tuple-element.15.acc_hbm, ...), custom_call_target="tpu_custom_call", output_to_operand_aliasing={{}: (6, {})} | custom-call | tf_op jit(solution)/shard_map/pallas_call | solution.py:317
  (6 shorter events, 0.0 us)
Async XLA Ops:
  0.0 7.4 %copy-start.1 = (s32[4]{0:T(128)S(1)}, s32[4]{0:T(128)}, u32[]{:S(2)}) copy-start(s32[4]{0:T(128)} %param.7) | copy-start | bytes 52
  0.0 21.7 %copy-start = (bf16[512,2,512]{2,1,0:T(2,128)(2,1)S(1)}, bf16[512,2,512]{2,1,0:T(2,128)(2,1)}, u32[]{:S(2)}) copy-start(bf16[512,2,512]{2,1,0:T(2,128)(2,1)} %param.4) | copy-start | bytes 3145732
  1.7 15.6 %collective-permute-start = (bf16[512,4,128]{2,1,0:T(4,128)(2,1)S(1)}, bf16[512,4,128]{2,1,0:T(4,128)(2,1)S(1)}, u32[]{:S(2)}, u32[]{:S(2)}) collective-permute-start(bf16[512,4,128]{2,1,0:T(4,128)(2,1)S(1)} %pad_maximum_fusion), channel_id=1, source_target_pairs={{0,4},{4,8},{8,12},{1,5},{5,9},{9,13},{2,6},{6,10},{10,14},{3,7},{... | collective-permute-start | bytes 1572872 | tf_op jit(solution)/shard_map/ppermute | solution.py:14
  17.4 22.8 %collective-permute-start.1 = (bf16[384,4,128]{2,1,0:T(4,128)(2,1)S(1)}, bf16[384,4,128]{2,1,0:T(4,128)(2,1)S(1)}, u32[]{:S(2)}, u32[]{:S(2)}) collective-permute-start(bf16[384,4,128]{2,1,0:T(4,128)(2,1)S(1)} %slice.20), channel_id=1, source_target_pairs={{0,4},{4,8},{8,12},{1,5},{5,9},{9,13},{2,6},{6,10},{10,14},{3,7},{... | collective-permute-start | bytes 1179656 | tf_op jit(solution)/shard_map/ppermute | solution.py:14

commit v11 on v8

--- a/solution.py
+++ b/solution.py
@@ -34,7 +34,7 @@
     return regions
 
 
-def make_stage(stage, first, last, provisional, dev_blocks, doc_blk, firsts, groups, head_dim, score_scale):
+def make_stage(stage, first, last, provisional, blocked, dev_blocks, doc_blk, firsts, groups, head_dim, score_scale):
     def local_index(rel):
         if stage == 0:
             return rel
@@ -59,24 +59,31 @@
             acc_out, m_out, l_out = rest[:3]
             (s_sc,) = rest[3:]
 
-        for i in range(dev_blocks):
+        steps = [(pl.program_id(1), 0)] if blocked else [(i, i) for i in range(dev_blocks)]
+        for i, qb in steps:
             start = rel_ref[i]
-            regions = stage_regions(stage, i, dev_blocks, doc_blk, firsts)
+            regions = stage_regions(stage, qb, dev_blocks, doc_blk, firsts)
 
             def finish(m_new, row_sum, acc):
                 if last or provisional:
                     out = jnp.transpose(acc * (1.0 / row_sum))
                     for g in range(groups):
-                        o_ref[i * BLK : (i + 1) * BLK, g * head_dim : (g + 1) * head_dim] = out[
+                        o_ref[qb * BLK : (qb + 1) * BLK, g * head_dim : (g + 1) * head_dim] = out[
                             g * BLK : (g + 1) * BLK
                         ].astype(o_ref.dtype)
                 if not last:
-                    acc_out[i] = acc
-                    m_out[i : i + 1, :] = m_new
-                    l_out[i : i + 1, :] = row_sum
+                    if blocked:
+                        acc_out[...] = acc
+                    else:
+                        acc_out[i] = acc
+                    m_out[pl.ds(i, 1), :] = m_new
+                    l_out[pl.ds(i, 1), :] = row_sum
+
+            def acc_old():
+                return acc_in[...] if blocked else acc_in[i]
 
             def passthrough():
-                finish(m_in[i : i + 1, :], l_in[i : i + 1, :], acc_in[i])
+                finish(m_in[pl.ds(i, 1), :], l_in[pl.ds(i, 1), :], acc_old())
 
             if not regions:
                 passthrough()
@@ -84,7 +91,7 @@
 
             def compute():
                 q = jnp.concatenate(
-                    [q_ref[i * BLK : (i + 1) * BLK, g * head_dim : (g + 1) * head_dim] for g in range(groups)],
+                    [q_ref[qb * BLK : (qb + 1) * BLK, g * head_dim : (g + 1) * head_dim] for g in range(groups)],
                     axis=0,
                 )
                 m_blk = None
@@ -96,7 +103,7 @@
                     ) * score_scale
                     key = lax.broadcasted_iota(jnp.int32, sc.shape, 0) // BLK + rels[0]
                     keep = key >= start
-                    if rels[-1] == i:
+                    if stage == 0 and rels[-1] == qb:
                         key_pos = lax.broadcasted_iota(jnp.int32, sc.shape, 0) + (rels[0] - i) * BLK
                         tok = lax.broadcasted_iota(jnp.int32, sc.shape, 1) % BLK
                         keep = keep & (key_pos <= tok)
@@ -109,11 +116,11 @@
                     row_sum = jnp.zeros(m_new.shape, jnp.float32)
                     acc = jnp.zeros((head_dim, groups * BLK), jnp.float32)
                 else:
-                    m_old = m_in[i : i + 1, :]
+                    m_old = m_in[pl.ds(i, 1), :]
                     m_new = jnp.maximum(m_old, m_blk)
                     alpha = jnp.exp(m_old - m_new)
-                    row_sum = alpha * l_in[i : i + 1, :]
-                    acc = alpha * acc_in[i]
+                    row_sum = alpha * l_in[pl.ds(i, 1), :]
+                    acc = alpha * acc_old()
                 for r, rels in enumerate(regions):
                     p = jnp.exp(s_sc[r, : len(rels) * BLK, :] - m_new)
                     row_sum = row_sum + jnp.sum(p, axis=0, keepdims=True)
@@ -282,26 +289,45 @@
         first = stage == 0
         last = False
         provisional = stage == reach - 1
-        kernel = make_stage(stage, first, last, provisional, dev_blocks, doc_blk, firsts, groups, head_dim, score_scale)
-        kv_spec = pl.BlockSpec((2, kv_src[stage].shape[1], head_dim), lambda h, rel: (0, 0, h))
-        in_specs = [q_spec, kv_spec] + ([] if first else state_specs)
+        blocked = not first and all(
+            stage_regions(stage, i, dev_blocks, doc_blk, firsts) == stage_regions(stage, 0, dev_blocks, doc_blk, firsts)
+            for i in range(dev_blocks)
+        )
+        kernel = make_stage(stage, first, last, provisional, blocked, dev_blocks, doc_blk, firsts, groups, head_dim, score_scale)
+        if blocked:
+            grid = (heads, dev_blocks)
+            q_sp = pl.BlockSpec((BLK, qwidth), lambda h, i, rel: (i, h))
+            kv_spec = pl.BlockSpec((2, kv_src[stage].shape[1], head_dim), lambda h, i, rel: (0, 0, h))
+            st_specs = [
+                pl.BlockSpec((None, None, head_dim, rows), lambda h, i, rel: (h, i, 0, 0)),
+                pl.BlockSpec((None, dev_blocks, rows), lambda h, i, rel: (h, 0, 0)),
+                pl.BlockSpec((None, dev_blocks, rows), lambda h, i, rel: (h, 0, 0)),
+            ]
+            sem = ("arbitrary", "arbitrary")
+        else:
+            grid = (heads,)
+            q_sp = q_spec
+            kv_spec = pl.BlockSpec((2, kv_src[stage].shape[1], head_dim), lambda h, rel: (0, 0, h))
+            st_specs = state_specs
+            sem = ("arbitrary",)
+        in_specs = [q_sp, kv_spec] + ([] if first else st_specs)
         args = [rel_start, q2, kv_src[stage]] + ([] if first else list(state))
         out_shape = state_shapes
-        out_specs = state_specs
+        out_specs = st_specs
         if provisional:
             out_shape = state_shapes + (jax.ShapeDtypeStruct((tok_rows, heads * qwidth), queries.dtype),)
-            out_specs = state_specs + [q_spec]
+            out_specs = st_specs + [q_sp]
         res = pl.pallas_call(
             kernel,
             out_shape=out_shape,
             grid_spec=pltpu.PrefetchScalarGridSpec(
                 num_scalar_prefetch=1,
-                grid=(heads,),
+                grid=grid,
                 in_specs=in_specs,
                 out_specs=out_specs,
                 scratch_shapes=scratch,
             ),
-            compiler_params=pltpu.CompilerParams(dimension_semantics=("arbitrary",)),
+            compiler_params=pltpu.CompilerParams(dimension_semantics=sem),
         )(*args)
         state = res[:3]
         if provisional:

time: 45.9 us -> 48.2 us (1.050)
  Pallas kernels: 18.8 us -> 21 us
    pallas_call x2, Pallas kernels: 13.1 us -> 15.3 us  [on_device(): pl.pallas_call(kernel, out_shape=out_shape, grid_spec=pltpu.PrefetchScala...]
  transfers between devices with their start and end apart: 2 -> 2, of which waited for: 1 -> 1; matrix products, arithmetic and copies ran while one was open for 10% -> 10% of each run, Pallas kernels for 29% -> 32%
where the time goes in v11:
time: 48.2 us; the launch traced here: 47.8 us
  Pallas kernels  21 us (44%)
  waiting for transfers between devices  11.9 us (25%)
  local copies, waits for them, and re-layouts  7 us (15%)
  starting transfers between devices  6.97 us (14%)
  other arithmetic  0.89 us (2%)
    pallas_call x2, Pallas kernels, on_device(): pl.pallas_call(kernel, out_shape=out_shape, grid_spec=pltpu.PrefetchScala...  15.3 us
    ppermute x2, waiting for transfers between devices, shift_up(): return lax.ppermute(block, axis, [(i, i + 1) for i in range(size - 1)])  11.9 us
    ppermute x2, starting transfers between devices, shift_up(): return lax.ppermute(block, axis, [(i, i + 1) for i in range(size - 1)])  6.97 us
    pallas_call x1, Pallas kernels, on_device(): pl.pallas_call(make_patch(reach, heads, dev_blocks, doc_blk, firsts, grou...  5.69 us
    reshape x1, local copies, waits for them, and re-layouts, on_device(): out = res[3].reshape(tok_rows, heads, qwidth)  2.62 us
    another operation x3, local copies, waits for them, and re-layouts, on_device(): kv_cur = jnp.stack([k2, v2])  2.35 us
    unnamed x12, local copies, waits for them, and re-layouts  2 us
  transfers between devices with their start and end apart: 2, of which 1 were waited for; matrix products, arithmetic and copies ran while one was open for 10% of the time, Pallas kernels for 32%

profile of v11, /device:TPU:18, one launch (start us, length us, event | category | flops | bytes accessed | tf_op | source)
XLA Modules:
  0.0 47.8 jit_solution(16671972091554034611)
XLA Ops:
  0.0 0.0 copy-start.4
  0.0 0.0 copy-start.2
  0.0 1.2 %stack_reshape.6 = bf16[1,512,256]{2,1,0:T(8,128)(2,1)S(1)} reshape(bf16[512,2,128]{2,1,0:T(2,128)(2,1)} %param.5) | data formatting | bytes 524288 | tf_op jit(solution)/shard_map/stack;reshape | solution.py:262
  1.2 1.1 %stack_reshape.7 = bf16[1,512,256]{2,1,0:T(8,128)(2,1)S(1)} reshape(bf16[512,2,128]{2,1,0:T(2,128)(2,1)} %param.6) | data formatting | bytes 524288 | tf_op jit(solution)/shard_map/stack;reshape | solution.py:262
  2.4 0.0 copy-start.1
  2.4 3.5 %collective-permute-start = (bf16[2,512,256]{2,1,0:T(8,128)(2,1)S(1)}, bf16[2,512,256]{2,1,0:T(8,128)(2,1)S(1)}, u32[]{:S(2)}, u32[]{:S(2)}) collective-permute-start(bf16[2,512,256]{2,1,0:T(8,128)(2,1)S(1)} %constant_dynamic-update-slice_fusion.kv_ref), channel_id=1, source_target_pairs={{0,4},{4,8},{8,12},{1,5},{5,9},{9,13},{2,6},{6,10},{10,14},{3,7},{... | collective-permute-start | bytes 1572872 | tf_op jit(solution)/shard_map/ppermute | solution.py:14
  5.9 0.0 copy-done.4
  5.9 0.2 reduce-window.9
  6.1 11.9 %collective-permute-done.kv_ref = bf16[2,512,256]{2,1,0:T(8,128)(2,1)S(1)} collective-permute-done((bf16[2,512,256]{2,1,0:T(8,128)(2,1)S(1)}, bf16[2,512,256]{2,1,0:T(8,128)(2,1)S(1)}, u32[]{:S(2)}, u32[]{:S(2)}) %collective-permute-start) | collective-permute-done | bytes 524320 | tf_op jit(solution)/shard_map/ppermute | solution.py:14
  18.0 0.0 copy-start
  18.0 3.5 %collective-permute-start.1 = (bf16[2,384,256]{2,1,0:T(8,128)(2,1)S(1)}, bf16[2,384,256]{2,1,0:T(8,128)(2,1)S(1)}, u32[]{:S(2)}, u32[]{:S(2)}) collective-permute-start(bf16[2,384,256]{2,1,0:T(8,128)(2,1)S(1)} %slice.4), channel_id=1, source_target_pairs={{0,4},{4,8},{8,12},{1,5},{5,9},{9,13},{2,6},{6,10},{10,14},{3,7},{... | collective-permute-start | bytes 1179656 | tf_op jit(solution)/shard_map/ppermute | solution.py:14
  21.5 0.0 copy-done.2
  21.5 1.2 %copy.6 = bf16[64,8,2,512]{3,1,2,0:T(8,128)(2,1)} copy(bf16[64,8,2,512]{3,2,1,0:T(2,128)(2,1)S(1)} %bitcast.8) | data formatting | bytes 2097152
  22.7 0.2 select_reduce_fusion
  22.9 0.5 %broadcast_subtract_fusion.rel_ref = s32[4]{0:T(128)} fusion(s32[4]{0:T(128)S(1)} %select_reduce_fusion, s32[]{:T(128)S(6)} %mul.3), kind=kLoop, calls=%fused_computation.5 | loop fusion | flops 4 | bytes 36 | tf_op jit(solution)/shard_map/sub | solution.py:256
  23.5 0.0 copy-done.1
  23.5 6.3 %shard_map.46 = (f32[2,4,128,512]{3,2,1,0:T(8,128)}, f32[2,4,512]{2,1,0:T(4,128)}, f32[2,4,512]{2,1,0:T(4,128)}) custom-call(s32[4]{0:T(128)} %broadcast_subtract_fusion.rel_ref, bf16[512,1024]{1,0:T(8,128)(2,1)} %bitcast.5, bf16[2,512,256]{2,1,0:T(8,128)(2,1)} %copy-done.1), custom_call_target="tpu_custom_call" | custom-call | tf_op jit(solution)/shard_map/pallas_call | solution.py:320
  29.7 0.0 copy-done
  29.8 9.0 %shard_map.47 = (f32[2,4,128,512]{3,2,1,0:T(8,128)}, f32[2,4,512]{2,1,0:T(4,128)}, f32[2,4,512]{2,1,0:T(4,128)}, bf16[512,1024]{1,0:T(8,128)(2,1)}) custom-call(s32[4]{0:T(128)} %broadcast_subtract_fusion.rel_ref, bf16[512,1024]{1,0:T(8,128)(2,1)} %bitcast.6, bf16[2,512,256]{2,1,0:T(8,128)(2,1)} %copy-done, f32[2,4,128,512]{3,2,1,0:T(8,128)} %get-tuple-element.12.refs_0_, ...), custom_call_target="tpu_custom_call" | custom-call | tf_op jit(solution)/shard_map/pallas_call | solution.py:320
  38.8 2.6 %reshape.40.prov_hbm = bf16[512,2,512]{2,1,0:T(2,128)(2,1)} reshape(bf16[512,1024]{1,0:T(8,128)(2,1)} %get-tuple-element.18) | data formatting | bytes 2097152 | tf_op jit(solution)/shard_map/reshape | solution.py:334
  41.4 0.0 collective-permute-done.1.kv_hbm
  41.4 0.0 copy-start.3
  41.4 0.7 %copy-done.3 = bf16[2,384,256]{2,1,0:T(8,128)(2,1)} copy-done((bf16[2,384,256]{2,1,0:T(8,128)(2,1)}, bf16[2,384,256]{2,1,0:T(8,128)(2,1)S(1)}, u32[]{:S(2)}) %copy-start.3) | copy-done | bytes 393240
  42.1 5.7 %shard_map.48 = bf16[512,2,512]{2,1,0:T(2,128)(2,1)} custom-call(s32[4]{0:T(128)} %broadcast_subtract_fusion.rel_ref, bf16[512,1024]{1,0:T(8,128)(2,1)} %bitcast.7, bf16[2,384,256]{2,1,0:T(8,128)(2,1)} %copy-done.3, f32[2,4,128,512]{3,2,1,0:T(8,128)} %get-tuple-element.15.acc_hbm, ...), custom_call_target="tpu_custom_call", output_to_operand_aliasing={{}: (6, {})} | custom-call | tf_op jit(solution)/shard_map/pallas_call | solution.py:339
  (4 shorter events, 0.1 us)
Async XLA Ops:
  0.0 5.9 %copy-start.4 = (s32[4]{0:T(128)S(1)}, s32[4]{0:T(128)}, u32[]{:S(2)}) copy-start(s32[4]{0:T(128)} %param.7) | copy-start | bytes 52
  0.0 21.5 %copy-start.2 = (bf16[512,2,512]{2,1,0:T(2,128)(2,1)S(1)}, bf16[512,2,512]{2,1,0:T(2,128)(2,1)}, u32[]{:S(2)}) copy-start(bf16[512,2,512]{2,1,0:T(2,128)(2,1)} %param.4) | copy-start | bytes 3145732
  2.4 21.1 %copy-start.1 = (bf16[2,512,256]{2,1,0:T(8,128)(2,1)}, bf16[2,512,256]{2,1,0:T(8,128)(2,1)S(1)}, u32[]{:S(2)}) copy-start(bf16[2,512,256]{2,1,0:T(8,128)(2,1)S(1)} %constant_dynamic-update-slice_fusion.kv_ref) | copy-start | bytes 1572868
  2.4 15.6 %collective-permute-start = (bf16[2,512,256]{2,1,0:T(8,128)(2,1)S(1)}, bf16[2,512,256]{2,1,0:T(8,128)(2,1)S(1)}, u32[]{:S(2)}, u32[]{:S(2)}) collective-permute-start(bf16[2,512,256]{2,1,0:T(8,128)(2,1)S(1)} %constant_dynamic-update-slice_fusion.kv_ref), channel_id=1, source_target_pairs={{0,4},{4,8},{8,12},{1,5},{5,9},{9,13},{2,6},{6,10},{10,14},{3,7},{... | collective-permute-start | bytes 1572872 | tf_op jit(solution)/shard_map/ppermute | solution.py:14
  18.0 11.8 %copy-start = (bf16[2,512,256]{2,1,0:T(8,128)(2,1)}, bf16[2,512,256]{2,1,0:T(8,128)(2,1)S(1)}, u32[]{:S(2)}) copy-start(bf16[2,512,256]{2,1,0:T(8,128)(2,1)S(1)} %collective-permute-done.kv_ref) | copy-start | bytes 1572868
  18.0 23.4 %collective-permute-start.1 = (bf16[2,384,256]{2,1,0:T(8,128)(2,1)S(1)}, bf16[2,384,256]{2,1,0:T(8,128)(2,1)S(1)}, u32[]{:S(2)}, u32[]{:S(2)}) collective-permute-start(bf16[2,384,256]{2,1,0:T(8,128)(2,1)S(1)} %slice.4), channel_id=1, source_target_pairs={{0,4},{4,8},{8,12},{1,5},{5,9},{9,13},{2,6},{6,10},{10,14},{3,7},{... | collective-permute-start | bytes 1179656 | tf_op jit(solution)/shard_map/ppermute | solution.py:14
  41.4 0.7 %copy-start.3 = (bf16[2,384,256]{2,1,0:T(8,128)(2,1)}, bf16[2,384,256]{2,1,0:T(8,128)(2,1)S(1)}, u32[]{:S(2)}) copy-start(bf16[2,384,256]{2,1,0:T(8,128)(2,1)S(1)} %collective-permute-done.1.kv_hbm) | copy-start | bytes 1179652
